TPU v7x, 32 devices: a whole 2x2x4 slice. The times are simulated.
32 devices in a mesh: dp: 4 (over z), expert: 8 (over y, x, core).
Axes of the slice: x: 2, y: 2, z: 4, core: 2. Of those that a mesh axis runs over, the one named last changes fastest.
Arguments:
- tokens: bfloat16 [384, 4096], P('expert', 'dp'), may hold values from -6 to 6
- out_grad: bfloat16 [384, 4096], P('expert', 'dp'), may hold values from -6 to 6
- expert_ids: int32 [384, 8], P('expert'), may hold values from 0 to 63, all different within a row; in each aligned block of 48 rows (0 to 47, 48 to 95, ...) at most 12 rows name the same one
- route_weights: float32 [384, 8], P('expert'), may hold values from 0.05 to 1
- gate_weight: bfloat16 [64, 4096, 768], P('expert', 'dp'), may hold values from -0.09375 to 0.09375
- up_weight: bfloat16 [64, 4096, 768], P('expert', 'dp'), may hold values from -0.09375 to 0.09375
- down_weight: bfloat16 [64, 768, 4096], P('expert', None, 'dp'), may hold values from -0.21875 to 0.21875
Outputs:
- layer_out: bfloat16 [384, 4096], P('expert', 'dp')
- grad_tokens: bfloat16 [384, 4096], P('expert', 'dp')
- gate_grad: bfloat16 [64, 4096, 768], P('expert', 'dp')
- up_grad: bfloat16 [64, 4096, 768], P('expert', 'dp')
- down_grad: bfloat16 [64, 768, 4096], P('expert', None, 'dp')
Inputs may be any that keep to these rules, and one draw needn't show every extreme that they name: `expert_ids`: each row names 8 different experts. In the 48 rows of one index of the expert axis no expert is named more than 12 times, and in every draw some expert is named exactly 12 times there.
All inputs are finite; a program needn't handle non-finite values.
Results may differ from a plain program's by a relative error of at most 0.029.
Values may be sent and summed in bfloat16 or wider, within the bound.
No kernel may reach another device: no remote copies, remote signals or barrier semaphores. Data moves between devices by JAX's collectives and lax.ppermute only.
A program may use at most 128 MiB of HBM per device.

v0:
```python
import jax
import jax.numpy as jnp
from jax import lax
from jax.sharding import PartitionSpec as P


def swiglu_parts(gate_sum, up_sum, back_sum):
    logistic = jax.nn.sigmoid(gate_sum)
    activated = gate_sum * logistic
    hidden = (activated * up_sum).astype(jnp.bfloat16)
    gate_delta = (back_sum * up_sum * logistic * (1.0 + gate_sum * (1.0 - logistic))).astype(
        jnp.bfloat16
    )
    up_delta = (back_sum * activated).astype(jnp.bfloat16)
    return (hidden, gate_delta, up_delta)


def split_f32(value):
    high = value.astype(jnp.bfloat16)
    rest = value - high.astype(jnp.float32)
    middle = rest.astype(jnp.bfloat16)
    low = (rest - middle.astype(jnp.float32)).astype(jnp.bfloat16)
    return high, middle, low


def local(tokens, out_grad, expert_ids, route_weights, gate_weight, up_weight, down_weight):
    token_count, width_dev = tokens.shape
    per_token = expert_ids.shape[1]
    local_experts = gate_weight.shape[0]
    hidden_units = gate_weight.shape[2]
    sources = lax.axis_size("expert")
    experts = local_experts * sources
    capacity = 2 * token_count * per_token // experts
    slot_count = token_count * per_token
    me = lax.axis_index("expert")

    high, middle, low = split_f32(route_weights)
    route_cols = 4 * per_token
    pad_cols = (-route_cols) % 128
    packed = jnp.concatenate(
        [
            tokens,
            out_grad,
            expert_ids.astype(jnp.bfloat16),
            high,
            middle,
            low,
            jnp.zeros((token_count, pad_cols), jnp.bfloat16),
        ],
        axis=1,
    )
    gathered = lax.all_gather(packed, "expert", axis=0, tiled=True)
    feats = gathered[:, : 2 * width_dev]
    route_all = gathered[:, 2 * width_dev : 2 * width_dev + route_cols].astype(jnp.float32)
    ids_all = route_all[:, :per_token].astype(jnp.int32)
    w_all = (
        route_all[:, per_token : 2 * per_token] + route_all[:, 2 * per_token : 3 * per_token]
    ) + route_all[:, 3 * per_token :]
    all_tokens = sources * token_count

    flat_all = ids_all.reshape(sources, slot_count)
    position = jnp.arange(slot_count, dtype=jnp.int32)
    earlier = (flat_all[:, None, :] == flat_all[:, :, None]) & (
        position[None, None, :] < position[None, :, None]
    )
    rank_all = jnp.sum(earlier.astype(jnp.int32), axis=2)
    local_e = flat_all - me * local_experts
    is_local = (local_e >= 0) & (local_e < local_experts)
    src = jnp.arange(sources, dtype=jnp.int32)[:, None]
    row_count = local_experts * sources * capacity
    row_of = jnp.where(is_local, (local_e * sources + src) * capacity + rank_all, row_count)
    row_of = row_of.reshape(sources * slot_count)
    token_of = jnp.arange(sources * slot_count, dtype=jnp.int32) // per_token
    target = jnp.arange(row_count, dtype=jnp.int32)
    hit = target[:, None] == row_of[None, :]
    holder = jnp.sum(jnp.where(hit, token_of[None, :] + 1, 0), axis=1) - 1
    row_weight = jnp.sum(jnp.where(hit, w_all.reshape(-1)[None, :], 0.0), axis=1)
    select = (holder[:, None] == jnp.arange(all_tokens, dtype=jnp.int32)[None, :]).astype(
        jnp.bfloat16
    )
    picked = jnp.dot(select, feats, preferred_element_type=jnp.float32)
    x_in = picked[:, :width_dev].astype(jnp.bfloat16)
    dy_in = (row_weight[:, None] * picked[:, width_dev:]).astype(jnp.bfloat16)
    x_in = x_in.reshape(local_experts, sources * capacity, width_dev)
    dy_in = dy_in.reshape(local_experts, sources * capacity, width_dev)

    gate_part = jnp.einsum(
        "jrd,jdf->jrf", x_in, gate_weight, preferred_element_type=jnp.float32
    ).astype(jnp.bfloat16)
    up_part = jnp.einsum(
        "jrd,jdf->jrf", x_in, up_weight, preferred_element_type=jnp.float32
    ).astype(jnp.bfloat16)
    front = jnp.concatenate([gate_part, up_part], axis=2).reshape(row_count, 2 * hidden_units)
    front_sums = lax.psum_scatter(front, "dp", scatter_dimension=0, tiled=True)
    back_part = jnp.einsum(
        "jrd,jfd->jrf", dy_in, down_weight, preferred_element_type=jnp.float32
    ).astype(jnp.bfloat16)
    back_sums = lax.psum_scatter(
        back_part.reshape(row_count, hidden_units), "dp", scatter_dimension=0, tiled=True
    )
    front_sums = front_sums.astype(jnp.float32)
    hidden, gate_delta, up_delta = swiglu_parts(
        front_sums[:, :hidden_units], front_sums[:, hidden_units:], back_sums.astype(jnp.float32)
    )
    hidden = lax.all_gather(hidden, "dp", axis=0, tiled=True)
    deltas = lax.all_gather(
        jnp.concatenate([gate_delta, up_delta], axis=1), "dp", axis=0, tiled=True
    )
    expert_shape = (local_experts, sources, capacity, hidden_units)
    hidden = hidden.reshape(expert_shape)
    gate_delta = deltas[:, :hidden_units].reshape(expert_shape)
    up_delta = deltas[:, hidden_units:].reshape(expert_shape)
    in_tokens = x_in.reshape(local_experts, sources, capacity, width_dev)
    in_grads = dy_in.reshape(local_experts, sources, capacity, width_dev)

    buffer_rows = experts * capacity
    expert_out = jnp.einsum(
        "jscf,jfd->sjcd", hidden, down_weight, preferred_element_type=jnp.float32
    ).astype(jnp.bfloat16)
    out_back = lax.all_to_all(
        expert_out.reshape(buffer_rows, width_dev), "expert", split_axis=0, concat_axis=0, tiled=True
    )
    down_grad = jnp.einsum(
        "jscf,jscd->jfd", hidden, in_grads, preferred_element_type=jnp.float32
    ).astype(jnp.bfloat16)
    expert_back = (
        jnp.einsum("jscf,jdf->sjcd", gate_delta, gate_weight, preferred_element_type=jnp.float32)
        + jnp.einsum("jscf,jdf->sjcd", up_delta, up_weight, preferred_element_type=jnp.float32)
    ).astype(jnp.bfloat16)
    grad_back = lax.all_to_all(
        expert_back.reshape(buffer_rows, width_dev), "expert", split_axis=0, concat_axis=0, tiled=True
    )
    gate_grad = jnp.einsum(
        "jscd,jscf->jdf", in_tokens, gate_delta, preferred_element_type=jnp.float32
    ).astype(jnp.bfloat16)
    up_grad = jnp.einsum(
        "jscd,jscf->jdf", in_tokens, up_delta, preferred_element_type=jnp.float32
    ).astype(jnp.bfloat16)

    flat_ids = expert_ids.reshape(slot_count)
    earlier_local = (flat_ids[None, :] == flat_ids[:, None]) & (
        position[None, :] < position[:, None]
    )
    slot_rank = jnp.sum(earlier_local.astype(jnp.int32), axis=1)
    slot_place = (flat_ids * capacity + slot_rank).reshape(token_count, per_token)
    picked_out = jnp.take(out_back, slot_place, axis=0).astype(jnp.float32)
    layer_out = jnp.sum(picked_out * route_weights[:, :, None], axis=1).astype(jnp.bfloat16)
    picked_back = jnp.take(grad_back, slot_place, axis=0).astype(jnp.float32)
    grad_tokens = jnp.sum(picked_back, axis=1).astype(jnp.bfloat16)
    return (layer_out, grad_tokens, gate_grad, up_grad, down_grad)


def solution(mesh):
    in_specs = (
        P("expert", "dp"),
        P("expert", "dp"),
        P("expert", None),
        P("expert", None),
        P("expert", "dp", None),
        P("expert", "dp", None),
        P("expert", None, "dp"),
    )
    out_specs = (
        P("expert", "dp"),
        P("expert", "dp"),
        P("expert", "dp", None),
        P("expert", "dp", None),
        P("expert", None, "dp"),
    )
    return jax.shard_map(local, mesh=mesh, in_specs=in_specs, out_specs=out_specs, check_vma=False)
```

profile of v0, /device:TPU:0, one launch (start us, length us, event | category | flops | bytes accessed | tf_op | source)
XLA Modules:
  0.0 285.5 jit_solution(7191488304311317399)
XLA Ops:
  9.1 1.7 concatenate.9
  10.9 28.8 %all-gather.4.cloned.1.call-done = bf16[384,2176]{1,0:T(8,128)(2,1)} async-done(((bf16[48,2176]{1,0:T(8,128)(2,1)}), bf16[384,2176]{1,0:T(8,128)(2,1)}) %all-gather.4.cloned.1.call-update) | async-done | bytes 1671184 | tf_op jit(solution)/shard_map/all_gather | solution.py:52
  41.5 1.6 convert_reduce_fusion
  44.5 1.8 fusion.12
  46.3 2.8 copy-done
  49.3 6.7 %convolution_convert_fusion.1 = bf16[8,96,768]{2,1,0:T(8,128)(2,1)S(1)} fusion(bf16[8,96,1024]{2,1,0:T(8,128)(2,1)S(1)} %bitcast.67, bf16[8,1024,768]{2,1,0:T(8,128)(2,1)} %param.14), kind=kOutput, calls=%fused_computation.26 | convolution fusion | flops 1208549376 | bytes 15335424 | tf_op jit(solution)/shard_map/jrd,jdf->jrf/dot_general | solution.py:90
  56.1 2.0 convolution_convert_fusion.2
  61.3 2.1 fusion.6
  63.5 10.0 %convolution_convert_fusion = bf16[8,96,768]{2,1,0:T(8,128)(2,1)} fusion(bf16[8,96,1024]{2,1,0:T(8,128)(2,1)S(1)} %bitcast.69, bf16[8,768,1024]{2,1,0:T(8,128)(2,1)} %param.15), kind=kOutput, calls=%fused_computation.25 | convolution fusion | flops 1208549376 | bytes 15335424 | tf_op jit(solution)/shard_map/jrd,jfd->jrf/dot_general | solution.py:95
  73.6 34.4 %reduce-scatter.3.cloned.1.call-done = bf16[192,1536]{1,0:T(8,128)(2,1)} async-done(((bf16[768,1536]{1,0:T(8,128)(2,1)}), bf16[192,1536]{1,0:T(8,128)(2,1)}) %reduce-scatter.3.cloned.1.call-update) | async-done | bytes 589840 | tf_op jit(solution)/shard_map/reduce_scatter | solution.py:94
  108.0 2.2 convert_element_type.99
  110.2 29.4 %reduce-scatter.5.cloned.1.call-done = bf16[192,768]{1,0:T(8,128)(2,1)} async-done(((bf16[768,768]{1,0:T(8,128)(2,1)}), bf16[192,768]{1,0:T(8,128)(2,1)}) %reduce-scatter.5.cloned.1.call-update) | async-done | bytes 294928 | tf_op jit(solution)/shard_map/reduce_scatter | solution.py:98
  139.6 2.5 fusion.17
  147.0 24.4 %all-gather.6.cloned.1.call-done = bf16[768,768]{1,0:T(8,128)(2,1)} async-done(((bf16[192,768]{1,0:T(8,128)(2,1)}), bf16[768,768]{1,0:T(8,128)(2,1)}) %all-gather.6.cloned.1.call-update) | async-done | bytes 1179664 | tf_op jit(solution)/shard_map/all_gather | solution.py:105
  171.4 2.2 reshape.122
  173.6 6.4 %convert_bitcast_fusion = bf16[8,8,12,1024]{3,2,0,1:T(8,128)(2,1)S(1)} fusion(bf16[8,8,12,768]{3,2,1,0:T(8,128)(2,1)S(1)} %reshape.122, bf16[8,768,1024]{2,1,0:T(8,128)(2,1)} %param.15), kind=kOutput, calls=%fused_computation.21 | convolution fusion | flops 1208745984 | bytes 15335424 | tf_op jit(solution)/shard_map/jscf,jfd->sjcd/dot_general | solution.py:117
  180.9 2.0 copy.63
  182.9 3.8 %all-to-all-start = ((bf16[8,96,1024]{2,1,0:T(8,128)(2,1)}), bf16[8,96,1024]{2,1,0:T(8,128)(2,1)S(1)}, u32[]{:S(2)}, u32[]{:S(2)}) async-start(bf16[8,96,1024]{2,1,0:T(8,128)(2,1)} %copy.63), calls=%async_computation.1 | async-start | bytes 3145728 | tf_op jit(solution)/shard_map/all_to_all | solution.py:120
  186.7 8.3 %bitcast_convert_fusion = bf16[8,768,1024]{2,1,0:T(8,128)(2,1)} fusion(bf16[8,8,12,768]{3,2,1,0:T(8,128)(2,1)S(1)} %reshape.122, bf16[8,8,12,1024]{3,2,1,0:T(8,128)(2,1)} %reshape_reshape.7), kind=kOutput, calls=%fused_computation.2 | convolution fusion | flops 1214251008 | bytes 15335424 | tf_op jit(solution)/shard_map/jscf,jscd->jfd/dot_general | solution.py:123
  195.0 12.5 %all-to-all-done = bf16[8,96,1024]{2,1,0:T(8,128)(2,1)S(1)} async-done(((bf16[8,96,1024]{2,1,0:T(8,128)(2,1)}), bf16[8,96,1024]{2,1,0:T(8,128)(2,1)S(1)}, u32[]{:S(2)}, u32[]{:S(2)}) %all-to-all-start) | async-done | bytes 1572896 | tf_op jit(solution)/shard_map/all_to_all | solution.py:120
  207.6 2.1 gather_fusion
  210.9 11.6 %all-gather.8.cloned.1.call-done = bf16[768,1536]{1,0:T(8,128)(2,1)} async-done(((bf16[192,1536]{1,0:T(8,128)(2,1)}), bf16[768,1536]{1,0:T(8,128)(2,1)}) %all-gather.8.cloned.1.call-update) | async-done | bytes 2359312 | tf_op jit(solution)/shard_map/all_gather | solution.py:106
  222.5 1.8 fusion.26
  226.8 9.1 %fusion = f32[8,8,12,1024]{3,2,1,0:T(8,128)S(1)} fusion(bf16[8,8,12,768]{3,2,1,0:T(8,128)(2,1)} %reshape.126, bf16[8,1024,768]{2,1,0:T(8,128)(2,1)} %param.14), kind=kOutput, calls=%fused_computation.5 | convolution fusion | flops 1207959552 | bytes 16908288 | tf_op jit(solution)/shard_map/jscf,jdf->sjcd/dot_general | solution.py:128
  236.0 10.6 %fusion.7 = bf16[8,8,12,1024]{3,2,0,1:T(8,128)(2,1)} fusion(f32[8,8,12,1024]{3,2,1,0:T(8,128)S(1)} %fusion, bf16[8,8,12,768]{3,2,1,0:T(8,128)(2,1)} %reshape.125, bf16[8,1024,768]{2,1,0:T(8,128)(2,1)} %param.13), kind=kOutput, calls=%fused_computation.20 | convolution fusion | flops 1209532416 | bytes 18481152 | tf_op jit(solution)/shard_map/jscf,jdf->sjcd/dot_general | solution.py:127
  246.5 2.5 copy.67
  249.0 2.0 copy.68
  251.1 4.0 %all-to-all-start.1 = ((bf16[8,96,1024]{2,1,0:T(8,128)(2,1)}), bf16[8,96,1024]{2,1,0:T(8,128)(2,1)S(1)}, u32[]{:S(2)}, u32[]{:S(2)}) async-start(bf16[8,96,1024]{2,1,0:T(8,128)(2,1)} %copy.68), calls=%async_computation.3 | async-start | bytes 3145728 | tf_op jit(solution)/shard_map/all_to_all | solution.py:130
  255.1 10.5 %bitcast_convert_fusion.2 = bf16[8,1024,768]{2,1,0:T(8,128)(2,1)} fusion(bf16[8,8,12,1024]{3,2,1,0:T(8,128)(2,1)} %reshape_reshape.6, bf16[8,8,12,768]{3,2,1,0:T(8,128)(2,1)S(1)} %copy-done.1), kind=kOutput, calls=%fused_computation.4 | convolution fusion | flops 1214251008 | bytes 15335424 | tf_op jit(solution)/shard_map/jscd,jscf->jdf/dot_general | solution.py:133
  265.6 6.8 %bitcast_convert_fusion.1 = bf16[8,1024,768]{2,1,0:T(8,128)(2,1)} fusion(bf16[8,8,12,1024]{3,2,1,0:T(8,128)(2,1)S(1)} %copy-done.3, bf16[8,8,12,768]{3,2,1,0:T(8,128)(2,1)S(1)} %copy-done.2), kind=kOutput, calls=%fused_computation.3 | convolution fusion | flops 1214251008 | bytes 15335424 | tf_op jit(solution)/shard_map/jscd,jscf->jdf/dot_general | solution.py:136
  272.4 3.5 %all-to-all-done.1 = bf16[8,96,1024]{2,1,0:T(8,128)(2,1)S(1)} async-done(((bf16[8,96,1024]{2,1,0:T(8,128)(2,1)}), bf16[8,96,1024]{2,1,0:T(8,128)(2,1)S(1)}, u32[]{:S(2)}, u32[]{:S(2)}) %all-to-all-start.1) | async-done | bytes 1572896 | tf_op jit(solution)/shard_map/all_to_all | solution.py:130
  275.9 2.1 gather_fusion.1
  (76 shorter events, 19.2 us)
Async XLA Ops:
  7.2 32.6 %all-gather.4.cloned.1.call-start = ((), (), s32[]{:S(2)}) async-start(), calls=%async_computation.4 | async-start | bytes 1880064 | tf_op jit(solution)/shard_map/all_gather | solution.py:52
  10.8 97.1 %reduce-scatter.3.cloned.1.call-start = ((), (), s32[]{:S(2)}) async-start(), calls=%async_computation.5 | async-start | bytes 2949120 | tf_op jit(solution)/shard_map/reduce_scatter | solution.py:94
  39.8 4.7 %copy-start.4 = (bf16[384,2176]{1,0:T(8,128)(2,1)S(1)}, bf16[384,2176]{1,0:T(8,128)(2,1)}, u32[]{:S(2)}) copy-start(bf16[384,2176]{1,0:T(8,128)(2,1)} %all-gather.4.cloned.1.call-done) | copy-start | bytes 5013508
  44.4 11.6 %slice-start = ((s8[12582912]{0:T(1024)(128)(4,1)}), s8[4194304]{0:T(1024)(128)(4,1)S(1)}, s32[]{:S(2)}) async-start(s8[12582912]{0:T(1024)(128)(4,1)} %bitcast.63), calls=%async_computation.9 | async-start | bytes 8388608
  44.4 11.6 %slice-start.1 = ((s8[12582912]{0:T(1024)(128)(4,1)}), s8[4194304]{0:T(1024)(128)(4,1)S(1)}, s32[]{:S(2)}) async-start(s8[12582912]{0:T(1024)(128)(4,1)} %bitcast.63), calls=%async_computation.10 | async-start | bytes 8388608
  46.3 2.8 copy-start
  49.3 6.7 %slice-start.2 = ((s8[12582912]{0:T(1024)(128)(4,1)}), s8[4194304]{0:T(1024)(128)(4,1)S(1)}, s32[]{:S(2)}) async-start(s8[12582912]{0:T(1024)(128)(4,1)} %bitcast.63), calls=%async_computation.11 | async-start | bytes 8388608
  59.8 79.8 %reduce-scatter.5.cloned.1.call-start = ((), (), s32[]{:S(2)}) async-start(), calls=%async_computation.7 | async-start | bytes 1474560 | tf_op jit(solution)/shard_map/reduce_scatter | solution.py:98
  73.5 68.7 %copy-start.7 = (f32[48,8]{0,1:T(8,128)S(1)}, f32[48,8]{0,1:T(8,128)}, u32[]{:S(2)}) copy-start(f32[48,8]{0,1:T(8,128)} %param.12) | copy-start | bytes 4612
  73.5 68.7 %copy-start.6 = (s32[48,8]{0,1:T(8,128)S(1)}, s32[48,8]{0,1:T(8,128)}, u32[]{:S(2)}) copy-start(s32[48,8]{0,1:T(8,128)} %param.11) | copy-start | bytes 4612
  73.5 97.9 %all-gather.6.cloned.1.call-start = ((), (), s32[]{:S(2)}) async-start(), calls=%async_computation.6 | async-start | bytes 1474560 | tf_op jit(solution)/shard_map/all_gather | solution.py:105
  142.1 80.4 %all-gather.8.cloned.1.call-start = ((), (), s32[]{:S(2)}) async-start(), calls=%async_computation.8 | async-start | bytes 2949120 | tf_op jit(solution)/shard_map/all_gather | solution.py:106
  144.6 1.5 copy-start.5
  182.9 24.7 %all-to-all-start = ((bf16[8,96,1024]{2,1,0:T(8,128)(2,1)}), bf16[8,96,1024]{2,1,0:T(8,128)(2,1)S(1)}, u32[]{:S(2)}, u32[]{:S(2)}) async-start(bf16[8,96,1024]{2,1,0:T(8,128)(2,1)} %copy.63), calls=%async_computation.1 | async-start | bytes 3145728 | tf_op jit(solution)/shard_map/all_to_all | solution.py:120
  251.1 4.0 %copy-start.1 = (bf16[8,8,12,768]{3,2,1,0:T(8,128)(2,1)S(1)}, bf16[8,8,12,768]{3,2,1,0:T(8,128)(2,1)}, u32[]{:S(2)}) copy-start(bf16[8,8,12,768]{3,2,1,0:T(8,128)(2,1)} %reshape.125) | copy-start | bytes 3538948
  251.1 24.8 %all-to-all-start.1 = ((bf16[8,96,1024]{2,1,0:T(8,128)(2,1)}), bf16[8,96,1024]{2,1,0:T(8,128)(2,1)S(1)}, u32[]{:S(2)}, u32[]{:S(2)}) async-start(bf16[8,96,1024]{2,1,0:T(8,128)(2,1)} %copy.68), calls=%async_computation.3 | async-start | bytes 3145728 | tf_op jit(solution)/shard_map/all_to_all | solution.py:130
  255.1 10.5 %copy-start.2 = (bf16[8,8,12,768]{3,2,1,0:T(8,128)(2,1)S(1)}, bf16[8,8,12,768]{3,2,1,0:T(8,128)(2,1)}, u32[]{:S(2)}) copy-start(bf16[8,8,12,768]{3,2,1,0:T(8,128)(2,1)} %reshape.126) | copy-start | bytes 3538948
  255.1 10.5 %copy-start.3 = (bf16[8,8,12,1024]{3,2,1,0:T(8,128)(2,1)S(1)}, bf16[8,8,12,1024]{3,2,1,0:T(8,128)(2,1)}, u32[]{:S(2)}) copy-start(bf16[8,8,12,1024]{3,2,1,0:T(8,128)(2,1)} %reshape_reshape.6) | copy-start | bytes 4718596
Sparse Core Ops, SparseCore 0:
  10.9 28.7 all-gather.3
  59.9 48.0 reduce-scatter.2
  110.8 28.6 reduce-scatter.4
  142.2 29.1 all-gather.5
  172.8 49.5 all-gather.7
where the time goes:
time: 286 us
  waiting for transfers between devices  145 us (51%)
  matrix products  72.3 us (25%)
  local copies, waits for them, and re-layouts  27.5 us (10%)
  other arithmetic  18.8 us (7%)
  between operations  14.1 us (5%)
  starting transfers between devices  8.16 us (3%)
    reduce_scatter x1, waiting for transfers between devices, local(): front_sums = lax.psum_scatter(front, 'dp', scatter_dimension=0, tiled=True)  34.4 us
    reduce_scatter x1, waiting for transfers between devices, local(): lax.psum_scatter(back_part.reshape(row_count, hidden_units), 'dp', scatte...  29.4 us
    all_gather x1, waiting for transfers between devices, local(): gathered = lax.all_gather(packed, 'expert', axis=0, tiled=True)  28.8 us
    all_gather x1, waiting for transfers between devices, local(): hidden = lax.all_gather(hidden, 'dp', axis=0, tiled=True)  24.4 us
    all_to_all x1, waiting for transfers between devices, local(): lax.all_to_all(expert_out.reshape(buffer_rows, width_dev), 'expert', spli...  12.5 us
    all_gather x1, waiting for transfers between devices, local(): lax.all_gather(jnp.concatenate([gate_delta, up_delta], axis=1), 'dp', axi...  11.6 us
    dot_general x1, matrix products, local(): jnp.einsum('jscf,jdf->sjcd', gate_delta, gate_weight, preferred_element_t...  10.6 us
    dot_general x1, matrix products, local(): jnp.einsum('jscd,jscf->jdf', in_tokens, gate_delta, preferred_element_typ...  10.5 us
  transfers between devices with their start and end apart: 7, of which 7 were waited for; matrix products, arithmetic and copies ran while one was open for 21% of the time, Pallas kernels for 0%

commit v1 on v0

--- a/solution.py
+++ b/solution.py
@@ -102,10 +102,11 @@
     hidden, gate_delta, up_delta = swiglu_parts(
         front_sums[:, :hidden_units], front_sums[:, hidden_units:], back_sums.astype(jnp.float32)
     )
-    hidden = lax.all_gather(hidden, "dp", axis=0, tiled=True)
     deltas = lax.all_gather(
         jnp.concatenate([gate_delta, up_delta], axis=1), "dp", axis=0, tiled=True
     )
+    hidden, deltas = lax.optimization_barrier((hidden, deltas))
+    hidden = lax.all_gather(hidden, "dp", axis=0, tiled=True)
     expert_shape = (local_experts, sources, capacity, hidden_units)
     hidden = hidden.reshape(expert_shape)
     gate_delta = deltas[:, :hidden_units].reshape(expert_shape)

time: 286 us -> 296 us (1.035)
  waiting for transfers between devices: 145 us -> 154 us
    all_gather x1, waiting for transfers between devices: 11.6 us -> 45.1 us  [local(): lax.all_gather(jnp.concatenate([gate_delta, up_delta], axis=1), 'dp', axi...]
    all_gather x1, waiting for transfers between devices: 24.4 us -> 0.01 us  [local(): hidden = lax.all_gather(hidden, 'dp', axis=0, tiled=True)]
  transfers between devices with their start and end apart: 7 -> 7, of which waited for: 7 -> 6; matrix products, arithmetic and copies ran while one was open for 21% -> 26% of each run, Pallas kernels for 0% -> 0%
where the time goes in v1:
time: 296 us; the launch traced here: 295 us
  waiting for transfers between devices  154 us (52%)
  matrix products  72.7 us (25%)
  local copies, waits for them, and re-layouts  27.5 us (9%)
  other arithmetic  18.7 us (6%)
  between operations  14.1 us (5%)
  starting transfers between devices  8.46 us (3%)
    all_gather x1, waiting for transfers between devices, local(): lax.all_gather(jnp.concatenate([gate_delta, up_delta], axis=1), 'dp', axi...  45.1 us
    reduce_scatter x1, waiting for transfers between devices, local(): front_sums = lax.psum_scatter(front, 'dp', scatter_dimension=0, tiled=True)  34.4 us
    reduce_scatter x1, waiting for transfers between devices, local(): lax.psum_scatter(back_part.reshape(row_count, hidden_units), 'dp', scatte...  29.4 us
    all_gather x1, waiting for transfers between devices, local(): gathered = lax.all_gather(packed, 'expert', axis=0, tiled=True)  28.8 us
    all_to_all x1, waiting for transfers between devices, local(): lax.all_to_all(expert_out.reshape(buffer_rows, width_dev), 'expert', spli...  12.3 us
    dot_general x1, matrix products, local(): jnp.einsum('jscf,jdf->sjcd', gate_delta, gate_weight, preferred_element_t...  10.6 us
    dot_general x1, matrix products, local(): jnp.einsum('jscd,jscf->jdf', in_tokens, gate_delta, preferred_element_typ...  10.5 us
    dot_general x1, matrix products, local(): jnp.einsum('jrd,jfd->jrf', dy_in, down_weight, preferred_element_type=jnp...  10 us
  transfers between devices with their start and end apart: 7, of which 6 were waited for; matrix products, arithmetic and copies ran while one was open for 26% of the time, Pallas kernels for 0%

profile of v1, /device:TPU:0, one launch (start us, length us, event | category | flops | bytes accessed | tf_op | source)
XLA Modules:
  0.0 295.1 jit_solution(1931625552168569829)
XLA Ops:
  9.1 1.7 concatenate.9
  10.9 28.8 %all-gather.4.cloned.1.call-done = bf16[384,2176]{1,0:T(8,128)(2,1)} async-done(((bf16[48,2176]{1,0:T(8,128)(2,1)}), bf16[384,2176]{1,0:T(8,128)(2,1)}) %all-gather.4.cloned.1.call-update) | async-done | bytes 1671184 | tf_op jit(solution)/shard_map/all_gather | solution.py:52
  41.5 1.6 convert_reduce_fusion
  44.5 1.8 fusion.12
  46.3 2.8 copy-done
  49.3 6.7 %convolution_convert_fusion.1 = bf16[8,96,768]{2,1,0:T(8,128)(2,1)S(1)} fusion(bf16[8,96,1024]{2,1,0:T(8,128)(2,1)S(1)} %bitcast.67, bf16[8,1024,768]{2,1,0:T(8,128)(2,1)} %param.14), kind=kOutput, calls=%fused_computation.26 | convolution fusion | flops 1208549376 | bytes 15335424 | tf_op jit(solution)/shard_map/jrd,jdf->jrf/dot_general | solution.py:90
  56.1 2.0 convolution_convert_fusion.2
  58.1 1.6 pad_maximum_fusion
  61.3 2.1 fusion.6
  63.5 10.0 %convolution_convert_fusion = bf16[8,96,768]{2,1,0:T(8,128)(2,1)} fusion(bf16[8,96,1024]{2,1,0:T(8,128)(2,1)S(1)} %bitcast.69, bf16[8,768,1024]{2,1,0:T(8,128)(2,1)} %param.15), kind=kOutput, calls=%fused_computation.25 | convolution fusion | flops 1208549376 | bytes 15335424 | tf_op jit(solution)/shard_map/jrd,jfd->jrf/dot_general | solution.py:95
  73.5 34.4 %reduce-scatter.3.cloned.1.call-done = bf16[192,1536]{1,0:T(8,128)(2,1)} async-done(((bf16[768,1536]{1,0:T(8,128)(2,1)}), bf16[192,1536]{1,0:T(8,128)(2,1)}) %reduce-scatter.3.cloned.1.call-update) | async-done | bytes 589840 | tf_op jit(solution)/shard_map/reduce_scatter | solution.py:94
  108.0 2.2 convert_element_type.99
  110.2 29.4 %reduce-scatter.5.cloned.1.call-done = bf16[192,768]{1,0:T(8,128)(2,1)} async-done(((bf16[768,768]{1,0:T(8,128)(2,1)}), bf16[192,768]{1,0:T(8,128)(2,1)}) %reduce-scatter.5.cloned.1.call-update) | async-done | bytes 294928 | tf_op jit(solution)/shard_map/reduce_scatter | solution.py:98
  139.6 2.4 fusion.17
  147.1 45.1 %all-gather.6.cloned.1.call-done = bf16[768,1536]{1,0:T(8,128)(2,1)} async-done(((bf16[192,1536]{1,0:T(8,128)(2,1)}), bf16[768,1536]{1,0:T(8,128)(2,1)}) %all-gather.6.cloned.1.call-update) | async-done | bytes 2359312 | tf_op jit(solution)/shard_map/all_gather | solution.py:105
  192.2 1.8 fusion.26
  196.6 9.4 %fusion = f32[8,8,12,1024]{3,2,1,0:T(8,128)S(1)} fusion(bf16[8,8,12,768]{3,2,1,0:T(8,128)(2,1)} %reshape.126, bf16[8,1024,768]{2,1,0:T(8,128)(2,1)} %param.14), kind=kOutput, calls=%fused_computation.5 | convolution fusion | flops 1207959552 | bytes 16908288 | tf_op jit(solution)/shard_map/jscf,jdf->sjcd/dot_general | solution.py:129
  206.1 10.6 %fusion.7 = bf16[8,8,12,1024]{3,2,0,1:T(8,128)(2,1)} fusion(f32[8,8,12,1024]{3,2,1,0:T(8,128)S(1)} %fusion, bf16[8,8,12,768]{3,2,1,0:T(8,128)(2,1)} %reshape.125, bf16[8,1024,768]{2,1,0:T(8,128)(2,1)} %param.13), kind=kOutput, calls=%fused_computation.20 | convolution fusion | flops 1209532416 | bytes 18481152 | tf_op jit(solution)/shard_map/jscf,jdf->sjcd/dot_general | solution.py:128
  216.7 2.5 copy.67
  219.2 2.0 copy.68
  221.2 4.0 %all-to-all-start.1 = ((bf16[8,96,1024]{2,1,0:T(8,128)(2,1)}), bf16[8,96,1024]{2,1,0:T(8,128)(2,1)S(1)}, u32[]{:S(2)}, u32[]{:S(2)}) async-start(bf16[8,96,1024]{2,1,0:T(8,128)(2,1)} %copy.68), calls=%async_computation.3 | async-start | bytes 3145728 | tf_op jit(solution)/shard_map/all_to_all | solution.py:131
  225.2 10.5 %bitcast_convert_fusion.2 = bf16[8,1024,768]{2,1,0:T(8,128)(2,1)} fusion(bf16[8,8,12,1024]{3,2,1,0:T(8,128)(2,1)} %reshape_reshape.6, bf16[8,8,12,768]{3,2,1,0:T(8,128)(2,1)S(1)} %copy-done.1), kind=kOutput, calls=%fused_computation.4 | convolution fusion | flops 1214251008 | bytes 15335424 | tf_op jit(solution)/shard_map/jscd,jscf->jdf/dot_general | solution.py:134
  235.7 6.8 %bitcast_convert_fusion.1 = bf16[8,1024,768]{2,1,0:T(8,128)(2,1)} fusion(bf16[8,8,12,1024]{3,2,1,0:T(8,128)(2,1)S(1)} %copy-done.3, bf16[8,8,12,768]{3,2,1,0:T(8,128)(2,1)S(1)} %copy-done.2), kind=kOutput, calls=%fused_computation.3 | convolution fusion | flops 1214251008 | bytes 15335424 | tf_op jit(solution)/shard_map/jscd,jscf->jdf/dot_general | solution.py:137
  242.5 3.5 %all-to-all-done.1 = bf16[8,96,1024]{2,1,0:T(8,128)(2,1)S(1)} async-done(((bf16[8,96,1024]{2,1,0:T(8,128)(2,1)}), bf16[8,96,1024]{2,1,0:T(8,128)(2,1)S(1)}, u32[]{:S(2)}, u32[]{:S(2)}) %all-to-all-start.1) | async-done | bytes 1572896 | tf_op jit(solution)/shard_map/all_to_all | solution.py:131
  246.0 2.1 gather_fusion.1
  249.2 2.2 reshape.124
  251.3 6.4 %convert_bitcast_fusion = bf16[8,8,12,1024]{3,2,0,1:T(8,128)(2,1)S(1)} fusion(bf16[8,8,12,768]{3,2,1,0:T(8,128)(2,1)S(1)} %reshape.124, bf16[8,768,1024]{2,1,0:T(8,128)(2,1)} %param.15), kind=kOutput, calls=%fused_computation.21 | convolution fusion | flops 1208745984 | bytes 15335424 | tf_op jit(solution)/shard_map/jscf,jfd->sjcd/dot_general | solution.py:118
  258.6 2.0 copy.63
  260.7 3.9 %all-to-all-start = ((bf16[8,96,1024]{2,1,0:T(8,128)(2,1)}), bf16[8,96,1024]{2,1,0:T(8,128)(2,1)S(1)}, u32[]{:S(2)}, u32[]{:S(2)}) async-start(bf16[8,96,1024]{2,1,0:T(8,128)(2,1)} %copy.63), calls=%async_computation.2 | async-start | bytes 3145728 | tf_op jit(solution)/shard_map/all_to_all | solution.py:121
  264.5 8.3 %bitcast_convert_fusion = bf16[8,768,1024]{2,1,0:T(8,128)(2,1)} fusion(bf16[8,8,12,768]{3,2,1,0:T(8,128)(2,1)S(1)} %reshape.124, bf16[8,8,12,1024]{3,2,1,0:T(8,128)(2,1)} %reshape_reshape.7), kind=kOutput, calls=%fused_computation.2 | convolution fusion | flops 1214251008 | bytes 15335424 | tf_op jit(solution)/shard_map/jscf,jscd->jfd/dot_general | solution.py:124
  272.9 12.3 %all-to-all-done = bf16[8,96,1024]{2,1,0:T(8,128)(2,1)S(1)} async-done(((bf16[8,96,1024]{2,1,0:T(8,128)(2,1)}), bf16[8,96,1024]{2,1,0:T(8,128)(2,1)S(1)}, u32[]{:S(2)}, u32[]{:S(2)}) %all-to-all-start) | async-done | bytes 1572896 | tf_op jit(solution)/shard_map/all_to_all | solution.py:121
  285.2 2.1 gather_fusion
  (74 shorter events, 17.8 us)
Async XLA Ops:
  7.2 32.6 %all-gather.4.cloned.1.call-start = ((), (), s32[]{:S(2)}) async-start(), calls=%async_computation.4 | async-start | bytes 1880064 | tf_op jit(solution)/shard_map/all_gather | solution.py:52
  10.8 97.1 %reduce-scatter.3.cloned.1.call-start = ((), (), s32[]{:S(2)}) async-start(), calls=%async_computation.5 | async-start | bytes 2949120 | tf_op jit(solution)/shard_map/reduce_scatter | solution.py:94
  39.8 4.7 %copy-start.4 = (bf16[384,2176]{1,0:T(8,128)(2,1)S(1)}, bf16[384,2176]{1,0:T(8,128)(2,1)}, u32[]{:S(2)}) copy-start(bf16[384,2176]{1,0:T(8,128)(2,1)} %all-gather.4.cloned.1.call-done) | copy-start | bytes 5013508
  44.4 11.6 %slice-start = ((s8[12582912]{0:T(1024)(128)(4,1)}), s8[4194304]{0:T(1024)(128)(4,1)S(1)}, s32[]{:S(2)}) async-start(s8[12582912]{0:T(1024)(128)(4,1)} %bitcast.63), calls=%async_computation.9 | async-start | bytes 8388608
  44.4 11.6 %slice-start.1 = ((s8[12582912]{0:T(1024)(128)(4,1)}), s8[4194304]{0:T(1024)(128)(4,1)S(1)}, s32[]{:S(2)}) async-start(s8[12582912]{0:T(1024)(128)(4,1)} %bitcast.63), calls=%async_computation.10 | async-start | bytes 8388608
  46.3 2.8 copy-start
  49.3 6.7 %slice-start.2 = ((s8[12582912]{0:T(1024)(128)(4,1)}), s8[4194304]{0:T(1024)(128)(4,1)S(1)}, s32[]{:S(2)}) async-start(s8[12582912]{0:T(1024)(128)(4,1)} %bitcast.63), calls=%async_computation.11 | async-start | bytes 8388608
  59.8 79.8 %reduce-scatter.5.cloned.1.call-start = ((), (), s32[]{:S(2)}) async-start(), calls=%async_computation.6 | async-start | bytes 1474560 | tf_op jit(solution)/shard_map/reduce_scatter | solution.py:98
  73.5 118.7 %all-gather.6.cloned.1.call-start = ((), (), s32[]{:S(2)}) async-start(), calls=%async_computation.7 | async-start | bytes 2949120 | tf_op jit(solution)/shard_map/all_gather | solution.py:105
  110.2 33.0 %copy-start.6 = (f32[48,8]{0,1:T(8,128)S(1)}, f32[48,8]{0,1:T(8,128)}, u32[]{:S(2)}) copy-start(f32[48,8]{0,1:T(8,128)} %param.12) | copy-start | bytes 4612
  110.2 33.1 %copy-start.5 = (s32[48,8]{0,1:T(8,128)S(1)}, s32[48,8]{0,1:T(8,128)}, u32[]{:S(2)}) copy-start(s32[48,8]{0,1:T(8,128)} %param.11) | copy-start | bytes 4612
  142.9 106.3 %all-gather.8.cloned.1.call-start = ((), (), s32[]{:S(2)}) async-start(), calls=%async_computation.8 | async-start | bytes 1474560 | tf_op jit(solution)/shard_map/all_gather | solution.py:109
  221.2 4.0 %copy-start.1 = (bf16[8,8,12,768]{3,2,1,0:T(8,128)(2,1)S(1)}, bf16[8,8,12,768]{3,2,1,0:T(8,128)(2,1)}, u32[]{:S(2)}) copy-start(bf16[8,8,12,768]{3,2,1,0:T(8,128)(2,1)} %reshape.125) | copy-start | bytes 3538948
  221.2 24.8 %all-to-all-start.1 = ((bf16[8,96,1024]{2,1,0:T(8,128)(2,1)}), bf16[8,96,1024]{2,1,0:T(8,128)(2,1)S(1)}, u32[]{:S(2)}, u32[]{:S(2)}) async-start(bf16[8,96,1024]{2,1,0:T(8,128)(2,1)} %copy.68), calls=%async_computation.3 | async-start | bytes 3145728 | tf_op jit(solution)/shard_map/all_to_all | solution.py:131
  225.2 10.5 %copy-start.2 = (bf16[8,8,12,768]{3,2,1,0:T(8,128)(2,1)S(1)}, bf16[8,8,12,768]{3,2,1,0:T(8,128)(2,1)}, u32[]{:S(2)}) copy-start(bf16[8,8,12,768]{3,2,1,0:T(8,128)(2,1)} %reshape.126) | copy-start | bytes 3538948
  225.2 10.5 %copy-start.3 = (bf16[8,8,12,1024]{3,2,1,0:T(8,128)(2,1)S(1)}, bf16[8,8,12,1024]{3,2,1,0:T(8,128)(2,1)}, u32[]{:S(2)}) copy-start(bf16[8,8,12,1024]{3,2,1,0:T(8,128)(2,1)} %reshape_reshape.6) | copy-start | bytes 4718596
  260.7 24.5 %all-to-all-start = ((bf16[8,96,1024]{2,1,0:T(8,128)(2,1)}), bf16[8,96,1024]{2,1,0:T(8,128)(2,1)S(1)}, u32[]{:S(2)}, u32[]{:S(2)}) async-start(bf16[8,96,1024]{2,1,0:T(8,128)(2,1)} %copy.63), calls=%async_computation.2 | async-start | bytes 3145728 | tf_op jit(solution)/shard_map/all_to_all | solution.py:121
Sparse Core Ops, SparseCore 0:
  10.9 28.7 all-gather.3
  59.9 48.0 reduce-scatter.2
  110.8 28.6 reduce-scatter.4
  143.0 49.1 all-gather.5
  193.6 29.2 all-gather.7

commit v2 on v0

--- a/solution.py
+++ b/solution.py
@@ -110,8 +110,7 @@
     hidden = hidden.reshape(expert_shape)
     gate_delta = deltas[:, :hidden_units].reshape(expert_shape)
     up_delta = deltas[:, hidden_units:].reshape(expert_shape)
-    in_tokens = x_in.reshape(local_experts, sources, capacity, width_dev)
-    in_grads = dy_in.reshape(local_experts, sources, capacity, width_dev)
+    rows_shape = (local_experts, sources * capacity, hidden_units)
 
     buffer_rows = experts * capacity
     expert_out = jnp.einsum(
@@ -121,7 +120,7 @@
         expert_out.reshape(buffer_rows, width_dev), "expert", split_axis=0, concat_axis=0, tiled=True
     )
     down_grad = jnp.einsum(
-        "jscf,jscd->jfd", hidden, in_grads, preferred_element_type=jnp.float32
+        "jrf,jrd->jfd", hidden.reshape(rows_shape), dy_in, preferred_element_type=jnp.float32
     ).astype(jnp.bfloat16)
     expert_back = (
         jnp.einsum("jscf,jdf->sjcd", gate_delta, gate_weight, preferred_element_type=jnp.float32)
@@ -131,10 +130,10 @@
         expert_back.reshape(buffer_rows, width_dev), "expert", split_axis=0, concat_axis=0, tiled=True
     )
     gate_grad = jnp.einsum(
-        "jscd,jscf->jdf", in_tokens, gate_delta, preferred_element_type=jnp.float32
+        "jrd,jrf->jdf", x_in, gate_delta.reshape(rows_shape), preferred_element_type=jnp.float32
     ).astype(jnp.bfloat16)
     up_grad = jnp.einsum(
-        "jscd,jscf->jdf", in_tokens, up_delta, preferred_element_type=jnp.float32
+        "jrd,jrf->jdf", x_in, up_delta.reshape(rows_shape), preferred_element_type=jnp.float32
     ).astype(jnp.bfloat16)
 
     flat_ids = expert_ids.reshape(slot_count)

time: 286 us -> 287 us (level)
  matrix products: 72.3 us -> 64.4 us
  waiting for transfers between devices: 145 us -> 151 us
    unnamed x24 -> x28, local copies, waits for them, and re-layouts: 3 us -> 7.75 us
    dot_general x1, matrix products: 6.71 us -> 1.98 us  [local(): jnp.einsum('jrd,jdf->jrf', x_in, up_weight, preferred_element_type=jnp.fl...]
    all_gather x1, waiting for transfers between devices: 24.4 us -> 28.4 us  [local(): hidden = lax.all_gather(hidden, 'dp', axis=0, tiled=True)]
    dot_general x3, matrix products: 25.6 us -> 22.5 us  [the longest x1 7.99 us: local(): jnp.einsum('jrd,jrf->jdf', x_in, up_delta.reshape(rows_shape), preferred_...]
    another operation x2 -> x0, local copies, waits for them, and re-layouts: 2.99 us -> none  [the longest x1 1.5 us: local(): in_tokens = x_in.reshape(local_experts, sources, capacity, width_dev)]
  transfers between devices with their start and end apart: 7 -> 7, of which waited for: 7 -> 7; matrix products, arithmetic and copies ran while one was open for 21% -> 19% of each run, Pallas kernels for 0% -> 0%
where the time goes in v2:
time: 287 us; the launch traced here: 286 us
  waiting for transfers between devices  151 us (53%)
  matrix products  64.4 us (22%)
  local copies, waits for them, and re-layouts  30 us (10%)
  other arithmetic  18.4 us (6%)
  between operations  14.1 us (5%)
  starting transfers between devices  8.29 us (3%)
    reduce_scatter x1, waiting for transfers between devices, local(): front_sums = lax.psum_scatter(front, 'dp', scatter_dimension=0, tiled=True)  34.4 us
    reduce_scatter x1, waiting for transfers between devices, local(): lax.psum_scatter(back_part.reshape(row_count, hidden_units), 'dp', scatte...  30.4 us
    all_gather x1, waiting for transfers between devices, local(): gathered = lax.all_gather(packed, 'expert', axis=0, tiled=True)  28.8 us
    all_gather x1, waiting for transfers between devices, local(): hidden = lax.all_gather(hidden, 'dp', axis=0, tiled=True)  28.4 us
    all_gather x1, waiting for transfers between devices, local(): lax.all_gather(jnp.concatenate([gate_delta, up_delta], axis=1), 'dp', axi...  12.7 us
    all_to_all x1, waiting for transfers between devices, local(): lax.all_to_all(expert_out.reshape(buffer_rows, width_dev), 'expert', spli...  12 us
    dot_general x1, matrix products, local(): jnp.einsum('jscf,jdf->sjcd', gate_delta, gate_weight, preferred_element_t...  10.6 us
    dot_general x1, matrix products, local(): jnp.einsum('jrd,jfd->jrf', dy_in, down_weight, preferred_element_type=jnp...  10 us
  transfers between devices with their start and end apart: 7, of which 7 were waited for; matrix products, arithmetic and copies ran while one was open for 19% of the time, Pallas kernels for 0%

profile of v2, /device:TPU:0, one launch (start us, length us, event | category | flops | bytes accessed | tf_op | source)
XLA Modules:
  0.0 285.8 jit_solution(10530870521209703146)
XLA Ops:
  9.1 1.7 concatenate.9
  10.9 28.8 %all-gather.4.cloned.1.call-done = bf16[384,2176]{1,0:T(8,128)(2,1)} async-done(((bf16[48,2176]{1,0:T(8,128)(2,1)}), bf16[384,2176]{1,0:T(8,128)(2,1)}) %all-gather.4.cloned.1.call-update) | async-done | bytes 1671184 | tf_op jit(solution)/shard_map/all_gather | solution.py:52
  44.5 1.8 fusion.12
  46.3 3.2 %copy-done.3 = f32[768,2048]{1,0:T(8,128)} copy-done((f32[768,2048]{1,0:T(8,128)}, f32[768,2048]{1,0:T(8,128)S(1)}, u32[]{:S(2)}) %copy-start.3) | copy-done | bytes 6291480
  49.8 2.1 copy-done
  51.8 2.0 convolution_convert_fusion.4
  55.7 2.0 convolution_convert_fusion.5
  60.8 2.1 fusion.6
  63.0 10.0 %convolution_convert_fusion.3 = bf16[8,96,768]{2,1,0:T(8,128)(2,1)} fusion(bf16[8,96,1024]{2,1,0:T(8,128)(2,1)S(1)} %bitcast.65, bf16[8,768,1024]{2,1,0:T(8,128)(2,1)} %param.15), kind=kOutput, calls=%fused_computation.25 | convolution fusion | flops 1208549376 | bytes 15335424 | tf_op jit(solution)/shard_map/jrd,jfd->jrf/dot_general | solution.py:95
  73.0 34.4 %reduce-scatter.3.cloned.1.call-done = bf16[192,1536]{1,0:T(8,128)(2,1)} async-done(((bf16[768,1536]{1,0:T(8,128)(2,1)}), bf16[192,1536]{1,0:T(8,128)(2,1)}) %reduce-scatter.3.cloned.1.call-update) | async-done | bytes 589840 | tf_op jit(solution)/shard_map/reduce_scatter | solution.py:94
  108.6 30.4 %reduce-scatter.5.cloned.1.call-done = bf16[192,768]{1,0:T(8,128)(2,1)} async-done(((bf16[768,768]{1,0:T(8,128)(2,1)}), bf16[192,768]{1,0:T(8,128)(2,1)}) %reduce-scatter.5.cloned.1.call-update) | async-done | bytes 294928 | tf_op jit(solution)/shard_map/reduce_scatter | solution.py:98
  139.1 2.0 fusion.17
  142.1 28.4 %all-gather.6.cloned.1.call-done = bf16[768,768]{1,0:T(8,128)(2,1)} async-done(((bf16[192,768]{1,0:T(8,128)(2,1)}), bf16[768,768]{1,0:T(8,128)(2,1)}) %all-gather.6.cloned.1.call-update) | async-done | bytes 1179664 | tf_op jit(solution)/shard_map/all_gather | solution.py:105
  170.4 2.2 reshape.122
  172.6 6.4 %convert_bitcast_fusion = bf16[8,8,12,1024]{3,2,0,1:T(8,128)(2,1)S(1)} fusion(bf16[8,8,12,768]{3,2,1,0:T(8,128)(2,1)S(1)} %reshape.122, bf16[8,768,1024]{2,1,0:T(8,128)(2,1)} %param.15), kind=kOutput, calls=%fused_computation.21 | convolution fusion | flops 1208745984 | bytes 15335424 | tf_op jit(solution)/shard_map/jscf,jfd->sjcd/dot_general | solution.py:116
  179.9 2.0 copy.63
  181.9 3.9 %all-to-all-start = ((bf16[8,96,1024]{2,1,0:T(8,128)(2,1)}), bf16[8,96,1024]{2,1,0:T(8,128)(2,1)S(1)}, u32[]{:S(2)}, u32[]{:S(2)}) async-start(bf16[8,96,1024]{2,1,0:T(8,128)(2,1)} %copy.63), calls=%async_computation.1 | async-start | bytes 3145728 | tf_op jit(solution)/shard_map/all_to_all | solution.py:119
  186.8 7.9 %convolution_convert_fusion = bf16[8,768,1024]{2,1,0:T(8,128)(2,1)} fusion(bf16[8,96,768]{2,1,0:T(8,128)(2,1)} %bitcast.73, bf16[8,96,1024]{2,1,0:T(8,128)(2,1)S(1)} %bitcast.66), kind=kOutput, calls=%fused_computation.11 | convolution fusion | flops 1214251008 | bytes 15335424 | tf_op jit(solution)/shard_map/jrf,jrd->jfd/dot_general | solution.py:122
  194.7 12.0 %all-to-all-done = bf16[8,96,1024]{2,1,0:T(8,128)(2,1)S(1)} async-done(((bf16[8,96,1024]{2,1,0:T(8,128)(2,1)}), bf16[8,96,1024]{2,1,0:T(8,128)(2,1)S(1)}, u32[]{:S(2)}, u32[]{:S(2)}) %all-to-all-start) | async-done | bytes 1572896 | tf_op jit(solution)/shard_map/all_to_all | solution.py:119
  206.7 2.7 gather_fusion
  209.4 12.7 %all-gather.8.cloned.1.call-done = bf16[768,1536]{1,0:T(8,128)(2,1)} async-done(((bf16[192,1536]{1,0:T(8,128)(2,1)}), bf16[768,1536]{1,0:T(8,128)(2,1)}) %all-gather.8.cloned.1.call-update) | async-done | bytes 2359312 | tf_op jit(solution)/shard_map/all_gather | solution.py:106
  222.1 1.8 fusion.26
  227.1 9.1 %fusion = f32[8,8,12,1024]{3,2,1,0:T(8,128)S(1)} fusion(bf16[8,8,12,768]{3,2,1,0:T(8,128)(2,1)} %reshape.126, bf16[8,1024,768]{2,1,0:T(8,128)(2,1)} %param.14), kind=kOutput, calls=%fused_computation.2 | convolution fusion | flops 1207959552 | bytes 16908288 | tf_op jit(solution)/shard_map/jscf,jdf->sjcd/dot_general | solution.py:127
  236.2 10.6 %fusion.7 = bf16[8,8,12,1024]{3,2,0,1:T(8,128)(2,1)} fusion(f32[8,8,12,1024]{3,2,1,0:T(8,128)S(1)} %fusion, bf16[8,8,12,768]{3,2,1,0:T(8,128)(2,1)} %reshape.125, bf16[8,1024,768]{2,1,0:T(8,128)(2,1)} %param.13), kind=kOutput, calls=%fused_computation.20 | convolution fusion | flops 1209532416 | bytes 18481152 | tf_op jit(solution)/shard_map/jscf,jdf->sjcd/dot_general | solution.py:126
  246.7 2.5 copy.67
  249.2 2.0 copy.68
  251.3 4.0 %all-to-all-start.1 = ((bf16[8,96,1024]{2,1,0:T(8,128)(2,1)}), bf16[8,96,1024]{2,1,0:T(8,128)(2,1)S(1)}, u32[]{:S(2)}, u32[]{:S(2)}) async-start(bf16[8,96,1024]{2,1,0:T(8,128)(2,1)} %copy.68), calls=%async_computation.3 | async-start | bytes 3145728 | tf_op jit(solution)/shard_map/all_to_all | solution.py:129
  255.2 2.4 multiply_reduce_fusion
  257.7 8.0 %convolution_convert_fusion.1 = bf16[8,1024,768]{2,1,0:T(8,128)(2,1)} fusion(bf16[8,96,1024]{2,1,0:T(8,128)(2,1)S(1)} %bitcast.61, bf16[8,96,768]{2,1,0:T(8,128)(2,1)} %bitcast.68), kind=kOutput, calls=%fused_computation.12 | convolution fusion | flops 1214251008 | bytes 15335424 | tf_op jit(solution)/shard_map/jrd,jrf->jdf/dot_general | solution.py:135
  265.7 6.6 %convolution_convert_fusion.2 = bf16[8,1024,768]{2,1,0:T(8,128)(2,1)} fusion(bf16[8,96,1024]{2,1,0:T(8,128)(2,1)S(1)} %bitcast.62, bf16[8,96,768]{2,1,0:T(8,128)(2,1)S(1)} %bitcast.67), kind=kOutput, calls=%fused_computation.13 | convolution fusion | flops 1214251008 | bytes 15335424 | tf_op jit(solution)/shard_map/jrd,jrf->jdf/dot_general | solution.py:132
  272.3 3.8 %all-to-all-done.1 = bf16[8,96,1024]{2,1,0:T(8,128)(2,1)S(1)} async-done(((bf16[8,96,1024]{2,1,0:T(8,128)(2,1)}), bf16[8,96,1024]{2,1,0:T(8,128)(2,1)S(1)}, u32[]{:S(2)}, u32[]{:S(2)}) %all-to-all-start.1) | async-done | bytes 1572896 | tf_op jit(solution)/shard_map/all_to_all | solution.py:129
  276.1 2.1 gather_fusion.1
  (78 shorter events, 20.1 us)
Async XLA Ops:
  7.2 32.6 %all-gather.4.cloned.1.call-start = ((), (), s32[]{:S(2)}) async-start(), calls=%async_computation.4 | async-start | bytes 1880064 | tf_op jit(solution)/shard_map/all_gather | solution.py:52
  10.8 96.6 %reduce-scatter.3.cloned.1.call-start = ((), (), s32[]{:S(2)}) async-start(), calls=%async_computation.5 | async-start | bytes 2949120 | tf_op jit(solution)/shard_map/reduce_scatter | solution.py:94
  39.8 4.7 %copy-start.7 = (bf16[384,2176]{1,0:T(8,128)(2,1)S(1)}, bf16[384,2176]{1,0:T(8,128)(2,1)}, u32[]{:S(2)}) copy-start(bf16[384,2176]{1,0:T(8,128)(2,1)} %all-gather.4.cloned.1.call-done) | copy-start | bytes 5013508
  44.4 7.4 %copy-start = (bf16[8,1024,768]{2,1,0:T(8,128)(2,1)S(1)}, bf16[8,1024,768]{2,1,0:T(8,128)(2,1)}, u32[]{:S(2)}) copy-start(bf16[8,1024,768]{2,1,0:T(8,128)(2,1)} %param.14) | copy-start | bytes 37748740
  44.4 9.4 %slice-start = ((s8[12582912]{0:T(1024)(128)(4,1)}), s8[4194304]{0:T(1024)(128)(4,1)S(1)}, s32[]{:S(2)}) async-start(s8[12582912]{0:T(1024)(128)(4,1)} %bitcast.57), calls=%async_computation.9 | async-start | bytes 8388608
  44.5 9.8 %slice-start.1 = ((s8[12582912]{0:T(1024)(128)(4,1)}), s8[4194304]{0:T(1024)(128)(4,1)S(1)}, s32[]{:S(2)}) async-start(s8[12582912]{0:T(1024)(128)(4,1)} %bitcast.57), calls=%async_computation.10 | async-start | bytes 8388608
  46.3 3.2 %copy-start.3 = (f32[768,2048]{1,0:T(8,128)}, f32[768,2048]{1,0:T(8,128)S(1)}, u32[]{:S(2)}) copy-start(f32[768,2048]{1,0:T(8,128)S(1)} %fusion.12) | copy-start | bytes 18874372
  49.8 4.1 %copy-start.1 = (bf16[768,1024]{1,0:T(8,128)(2,1)}, bf16[768,1024]{1,0:T(8,128)(2,1)S(1)}, u32[]{:S(2)}) copy-start(bf16[768,1024]{1,0:T(8,128)(2,1)S(1)} %slice.90) | copy-start | bytes 4718596
  51.8 3.8 %slice-start.2 = ((s8[12582912]{0:T(1024)(128)(4,1)}), s8[4194304]{0:T(1024)(128)(4,1)S(1)}, s32[]{:S(2)}) async-start(s8[12582912]{0:T(1024)(128)(4,1)} %bitcast.57), calls=%async_computation.11 | async-start | bytes 8388608
  59.3 79.8 %reduce-scatter.5.cloned.1.call-start = ((), (), s32[]{:S(2)}) async-start(), calls=%async_computation.7 | async-start | bytes 1474560 | tf_op jit(solution)/shard_map/reduce_scatter | solution.py:98
  73.0 97.4 %all-gather.6.cloned.1.call-start = ((), (), s32[]{:S(2)}) async-start(), calls=%async_computation.6 | async-start | bytes 1474560 | tf_op jit(solution)/shard_map/all_gather | solution.py:105
  141.1 80.9 %all-gather.8.cloned.1.call-start = ((), (), s32[]{:S(2)}) async-start(), calls=%async_computation.8 | async-start | bytes 2949120 | tf_op jit(solution)/shard_map/all_gather | solution.py:106
  181.9 3.9 %copy-start.9 = (f32[48,8]{0,1:T(8,128)S(1)}, f32[48,8]{0,1:T(8,128)}, u32[]{:S(2)}) copy-start(f32[48,8]{0,1:T(8,128)} %param.12) | copy-start | bytes 4612
  181.9 4.0 %copy-start.8 = (s32[48,8]{0,1:T(8,128)S(1)}, s32[48,8]{0,1:T(8,128)}, u32[]{:S(2)}) copy-start(s32[48,8]{0,1:T(8,128)} %param.11) | copy-start | bytes 4612
  181.9 24.8 %all-to-all-start = ((bf16[8,96,1024]{2,1,0:T(8,128)(2,1)}), bf16[8,96,1024]{2,1,0:T(8,128)(2,1)S(1)}, u32[]{:S(2)}, u32[]{:S(2)}) async-start(bf16[8,96,1024]{2,1,0:T(8,128)(2,1)} %copy.63), calls=%async_computation.1 | async-start | bytes 3145728 | tf_op jit(solution)/shard_map/all_to_all | solution.py:119
  223.8 1.5 copy-start.4
  223.9 1.9 copy-start.6
  251.3 6.4 %copy-start.2 = (bf16[768,1024]{1,0:T(8,128)(2,1)S(1)}, bf16[768,1024]{1,0:T(8,128)(2,1)}, u32[]{:S(2)}) copy-start(bf16[768,1024]{1,0:T(8,128)(2,1)} %copy-done.1) | copy-start | bytes 4718596
  251.3 24.8 %all-to-all-start.1 = ((bf16[8,96,1024]{2,1,0:T(8,128)(2,1)}), bf16[8,96,1024]{2,1,0:T(8,128)(2,1)S(1)}, u32[]{:S(2)}, u32[]{:S(2)}) async-start(bf16[8,96,1024]{2,1,0:T(8,128)(2,1)} %copy.68), calls=%async_computation.3 | async-start | bytes 3145728 | tf_op jit(solution)/shard_map/all_to_all | solution.py:129
  257.7 8.0 %copy-start.5 = (bf16[768,768]{1,0:T(8,128)(2,1)S(1)}, bf16[768,768]{1,0:T(8,128)(2,1)}, u32[]{:S(2)}) copy-start(bf16[768,768]{1,0:T(8,128)(2,1)} %copy-done.4) | copy-start | bytes 3538948
Sparse Core Ops, SparseCore 0:
  10.9 28.7 all-gather.3
  59.4 48.0 reduce-scatter.2
  110.3 28.6 reduce-scatter.4
  141.3 29.1 all-gather.5
  172.4 49.5 all-gather.7

commit v3 on v2

--- a/solution.py
+++ b/solution.py
@@ -34,29 +34,31 @@
     slot_count = token_count * per_token
     me = lax.axis_index("expert")
 
+    all_tokens = sources * token_count
+    least_cols = -(-1_050_000 // (2 * all_tokens))
     high, middle, low = split_f32(route_weights)
     route_cols = 4 * per_token
-    pad_cols = (-route_cols) % 128
-    packed = jnp.concatenate(
-        [
-            tokens,
-            out_grad,
-            expert_ids.astype(jnp.bfloat16),
-            high,
-            middle,
-            low,
-            jnp.zeros((token_count, pad_cols), jnp.bfloat16),
-        ],
-        axis=1,
+
+    def widened(parts):
+        cols = sum(part.shape[1] for part in parts)
+        wide = max(cols, least_cols)
+        wide = wide + (-wide) % 128
+        pad = jnp.zeros((token_count, wide - cols), jnp.bfloat16)
+        return jnp.concatenate(parts + [pad], axis=1)
+
+    gathered = lax.all_gather(
+        widened([tokens, expert_ids.astype(jnp.bfloat16), high, middle, low]),
+        "expert",
+        axis=0,
+        tiled=True,
     )
-    gathered = lax.all_gather(packed, "expert", axis=0, tiled=True)
-    feats = gathered[:, : 2 * width_dev]
-    route_all = gathered[:, 2 * width_dev : 2 * width_dev + route_cols].astype(jnp.float32)
+    tokens_all = gathered[:, :width_dev]
+    route_all = gathered[:, width_dev : width_dev + route_cols].astype(jnp.float32)
+    grads_all = lax.all_gather(widened([out_grad]), "expert", axis=0, tiled=True)[:, :width_dev]
     ids_all = route_all[:, :per_token].astype(jnp.int32)
     w_all = (
         route_all[:, per_token : 2 * per_token] + route_all[:, 2 * per_token : 3 * per_token]
     ) + route_all[:, 3 * per_token :]
-    all_tokens = sources * token_count
 
     flat_all = ids_all.reshape(sources, slot_count)
     position = jnp.arange(slot_count, dtype=jnp.int32)
@@ -78,9 +80,9 @@
     select = (holder[:, None] == jnp.arange(all_tokens, dtype=jnp.int32)[None, :]).astype(
         jnp.bfloat16
     )
-    picked = jnp.dot(select, feats, preferred_element_type=jnp.float32)
-    x_in = picked[:, :width_dev].astype(jnp.bfloat16)
-    dy_in = (row_weight[:, None] * picked[:, width_dev:]).astype(jnp.bfloat16)
+    x_in = jnp.dot(select, tokens_all, preferred_element_type=jnp.float32).astype(jnp.bfloat16)
+    picked_grad = jnp.dot(select, grads_all, preferred_element_type=jnp.float32)
+    dy_in = (row_weight[:, None] * picked_grad).astype(jnp.bfloat16)
     x_in = x_in.reshape(local_experts, sources * capacity, width_dev)
     dy_in = dy_in.reshape(local_experts, sources * capacity, width_dev)
 

time: 287 us -> 294 us (1.024)
  matrix products: 64.4 us -> 70.7 us
  waiting for transfers between devices: 151 us -> 157 us
  local copies, waits for them, and re-layouts: 30 us -> 25.6 us
    unnamed x28 -> x20, local copies, waits for them, and re-layouts: 7.75 us -> 2.1 us
    dot_general x1, matrix products: 1.98 us -> 7.38 us  [local(): jnp.einsum('jrd,jdf->jrf', x_in, up_weight, preferred_element_type=jnp.fl...]
    reduce_scatter x1, waiting for transfers between devices: 34.4 us -> 39.2 us  [local(): front_sums = lax.psum_scatter(front, 'dp', scatter_dimension=0, tiled=True)]
    all_gather x1 -> x2, waiting for transfers between devices: 28.8 us -> 31.1 us  [the longest x1 24.7 us: local(): lax.all_gather(widened([tokens, expert_ids.astype(jnp.bfloat16), high, mi...]
  transfers between devices with their start and end apart: 7 -> 8, of which waited for: 7 -> 8; matrix products, arithmetic and copies ran while one was open for 19% -> 25% of each run, Pallas kernels for 0% -> 0%
where the time goes in v3:
time: 294 us; the launch traced here: 293 us
  waiting for transfers between devices  157 us (53%)
  matrix products  70.7 us (24%)
  local copies, waits for them, and re-layouts  25.6 us (9%)
  other arithmetic  16.3 us (6%)
  between operations  14.4 us (5%)
  starting transfers between devices  8.33 us (3%)
    reduce_scatter x1, waiting for transfers between devices, local(): front_sums = lax.psum_scatter(front, 'dp', scatter_dimension=0, tiled=True)  39.2 us
    reduce_scatter x1, waiting for transfers between devices, local(): lax.psum_scatter(back_part.reshape(row_count, hidden_units), 'dp', scatte...  30.3 us
    all_gather x1, waiting for transfers between devices, local(): hidden = lax.all_gather(hidden, 'dp', axis=0, tiled=True)  28.4 us
    all_gather x1, waiting for transfers between devices, local(): lax.all_gather(widened([tokens, expert_ids.astype(jnp.bfloat16), high, mi...  24.7 us
    all_gather x1, waiting for transfers between devices, local(): lax.all_gather(jnp.concatenate([gate_delta, up_delta], axis=1), 'dp', axi...  12.6 us
    all_to_all x1, waiting for transfers between devices, local(): lax.all_to_all(expert_out.reshape(buffer_rows, width_dev), 'expert', spli...  12 us
    dot_general x1, matrix products, local(): jnp.einsum('jscf,jdf->sjcd', gate_delta, gate_weight, preferred_element_t...  10.6 us
    dot_general x1, matrix products, local(): jnp.einsum('jrd,jfd->jrf', dy_in, down_weight, preferred_element_type=jnp...  9.56 us
  transfers between devices with their start and end apart: 8, of which 8 were waited for; matrix products, arithmetic and copies ran while one was open for 25% of the time, Pallas kernels for 0%

profile of v3, /device:TPU:0, one launch (start us, length us, event | category | flops | bytes accessed | tf_op | source)
XLA Modules:
  0.0 292.8 jit_solution(10700788506385060523)
XLA Ops:
  9.1 1.7 concatenate.12
  12.5 24.7 %all-gather.5.cloned.1.call-done = bf16[384,1408]{1,0:T(8,128)(2,1)} async-done(((bf16[48,1408]{1,0:T(8,128)(2,1)}), bf16[384,1408]{1,0:T(8,128)(2,1)}) %all-gather.5.cloned.1.call-update) | async-done | bytes 1081360 | tf_op jit(solution)/shard_map/all_gather | solution.py:49
  39.0 1.6 convert_reduce_fusion
  42.9 7.4 %convolution_convert_fusion.5 = bf16[8,96,768]{2,1,0:T(8,128)(2,1)S(1)} fusion(bf16[8,96,1024]{2,1,0:T(8,128)(2,1)S(1)} %bitcast.59, bf16[8,1024,768]{2,1,0:T(8,128)(2,1)} %param.14), kind=kOutput, calls=%fused_computation.23 | convolution fusion | flops 1208549376 | bytes 15335424 | tf_op jit(solution)/shard_map/jrd,jdf->jrf/dot_general | solution.py:92
  51.8 2.0 convolution_convert_fusion.6
  53.8 1.6 pad_maximum_fusion
  57.0 6.4 %all-gather.9.cloned.1.call-done = bf16[384,1408]{1,0:T(8,128)(2,1)} async-done(((bf16[48,1408]{1,0:T(8,128)(2,1)}), bf16[384,1408]{1,0:T(8,128)(2,1)}) %all-gather.9.cloned.1.call-update) | async-done | bytes 1081360 | tf_op jit(solution)/shard_map/all_gather | solution.py:57
  63.4 2.2 multiply_convert_fusion
  65.6 9.6 %convolution_convert_fusion.4 = bf16[8,96,768]{2,1,0:T(8,128)(2,1)} fusion(bf16[8,96,1024]{2,1,0:T(8,128)(2,1)S(1)} %bitcast.66, bf16[8,768,1024]{2,1,0:T(8,128)(2,1)} %param.15), kind=kOutput, calls=%fused_computation.22 | convolution fusion | flops 1208549376 | bytes 15335424 | tf_op jit(solution)/shard_map/jrd,jfd->jrf/dot_general | solution.py:97
  75.2 39.2 %reduce-scatter.3.cloned.1.call-done = bf16[192,1536]{1,0:T(8,128)(2,1)} async-done(((bf16[768,1536]{1,0:T(8,128)(2,1)}), bf16[192,1536]{1,0:T(8,128)(2,1)}) %reduce-scatter.3.cloned.1.call-update) | async-done | bytes 589840 | tf_op jit(solution)/shard_map/reduce_scatter | solution.py:96
  115.5 30.3 %reduce-scatter.5.cloned.1.call-done = bf16[192,768]{1,0:T(8,128)(2,1)} async-done(((bf16[768,768]{1,0:T(8,128)(2,1)}), bf16[192,768]{1,0:T(8,128)(2,1)}) %reduce-scatter.5.cloned.1.call-update) | async-done | bytes 294928 | tf_op jit(solution)/shard_map/reduce_scatter | solution.py:100
  145.8 2.0 fusion.16
  148.8 28.4 %all-gather.7.cloned.1.call-done = bf16[768,768]{1,0:T(8,128)(2,1)} async-done(((bf16[192,768]{1,0:T(8,128)(2,1)}), bf16[768,768]{1,0:T(8,128)(2,1)}) %all-gather.7.cloned.1.call-update) | async-done | bytes 1179664 | tf_op jit(solution)/shard_map/all_gather | solution.py:107
  177.2 2.2 reshape.122
  179.3 6.4 %convert_bitcast_fusion = bf16[8,8,12,1024]{3,2,0,1:T(8,128)(2,1)S(1)} fusion(bf16[8,8,12,768]{3,2,1,0:T(8,128)(2,1)S(1)} %reshape.122, bf16[8,768,1024]{2,1,0:T(8,128)(2,1)} %param.15), kind=kOutput, calls=%fused_computation.19 | convolution fusion | flops 1208745984 | bytes 15335424 | tf_op jit(solution)/shard_map/jscf,jfd->sjcd/dot_general | solution.py:118
  186.7 2.0 copy.63
  188.7 3.9 %all-to-all-start = ((bf16[8,96,1024]{2,1,0:T(8,128)(2,1)}), bf16[8,96,1024]{2,1,0:T(8,128)(2,1)S(1)}, u32[]{:S(2)}, u32[]{:S(2)}) async-start(bf16[8,96,1024]{2,1,0:T(8,128)(2,1)} %copy.63), calls=%async_computation.1 | async-start | bytes 3145728 | tf_op jit(solution)/shard_map/all_to_all | solution.py:121
  193.6 7.9 %convolution_convert_fusion = bf16[8,768,1024]{2,1,0:T(8,128)(2,1)} fusion(bf16[8,96,768]{2,1,0:T(8,128)(2,1)} %bitcast.71, bf16[8,96,1024]{2,1,0:T(8,128)(2,1)S(1)} %bitcast.67), kind=kOutput, calls=%fused_computation.11 | convolution fusion | flops 1214251008 | bytes 15335424 | tf_op jit(solution)/shard_map/jrf,jrd->jfd/dot_general | solution.py:124
  201.5 12.0 %all-to-all-done = bf16[8,96,1024]{2,1,0:T(8,128)(2,1)S(1)} async-done(((bf16[8,96,1024]{2,1,0:T(8,128)(2,1)}), bf16[8,96,1024]{2,1,0:T(8,128)(2,1)S(1)}, u32[]{:S(2)}, u32[]{:S(2)}) %all-to-all-start) | async-done | bytes 1572896 | tf_op jit(solution)/shard_map/all_to_all | solution.py:121
  213.5 2.7 gather_fusion
  216.2 12.6 %all-gather.11.cloned.1.call-done = bf16[768,1536]{1,0:T(8,128)(2,1)} async-done(((bf16[192,1536]{1,0:T(8,128)(2,1)}), bf16[768,1536]{1,0:T(8,128)(2,1)}) %all-gather.11.cloned.1.call-update) | async-done | bytes 2359312 | tf_op jit(solution)/shard_map/all_gather | solution.py:108
  228.8 1.8 fusion.26
  233.8 9.1 %fusion = f32[8,8,12,1024]{3,2,1,0:T(8,128)S(1)} fusion(bf16[8,8,12,768]{3,2,1,0:T(8,128)(2,1)} %reshape.126, bf16[8,1024,768]{2,1,0:T(8,128)(2,1)} %param.14), kind=kOutput, calls=%fused_computation.2 | convolution fusion | flops 1207959552 | bytes 16908288 | tf_op jit(solution)/shard_map/jscf,jdf->sjcd/dot_general | solution.py:129
  242.9 10.6 %fusion.6 = bf16[8,8,12,1024]{3,2,0,1:T(8,128)(2,1)} fusion(f32[8,8,12,1024]{3,2,1,0:T(8,128)S(1)} %fusion, bf16[8,8,12,768]{3,2,1,0:T(8,128)(2,1)} %reshape.125, bf16[8,1024,768]{2,1,0:T(8,128)(2,1)} %param.13), kind=kOutput, calls=%fused_computation.18 | convolution fusion | flops 1209532416 | bytes 18481152 | tf_op jit(solution)/shard_map/jscf,jdf->sjcd/dot_general | solution.py:128
  253.5 2.5 copy.67
  255.9 2.0 copy.68
  258.0 4.0 %all-to-all-start.1 = ((bf16[8,96,1024]{2,1,0:T(8,128)(2,1)}), bf16[8,96,1024]{2,1,0:T(8,128)(2,1)S(1)}, u32[]{:S(2)}, u32[]{:S(2)}) async-start(bf16[8,96,1024]{2,1,0:T(8,128)(2,1)} %copy.68), calls=%async_computation.3 | async-start | bytes 3145728 | tf_op jit(solution)/shard_map/all_to_all | solution.py:131
  261.9 2.4 multiply_reduce_fusion
  264.4 8.0 %convolution_convert_fusion.1 = bf16[8,1024,768]{2,1,0:T(8,128)(2,1)} fusion(bf16[8,96,1024]{2,1,0:T(8,128)(2,1)S(1)} %bitcast.61, bf16[8,96,768]{2,1,0:T(8,128)(2,1)} %bitcast.64), kind=kOutput, calls=%fused_computation.12 | convolution fusion | flops 1214251008 | bytes 15335424 | tf_op jit(solution)/shard_map/jrd,jrf->jdf/dot_general | solution.py:137
  272.4 6.6 %convolution_convert_fusion.2 = bf16[8,1024,768]{2,1,0:T(8,128)(2,1)} fusion(bf16[8,96,1024]{2,1,0:T(8,128)(2,1)S(1)} %bitcast.62, bf16[8,96,768]{2,1,0:T(8,128)(2,1)S(1)} %bitcast.63), kind=kOutput, calls=%fused_computation.13 | convolution fusion | flops 1214251008 | bytes 15335424 | tf_op jit(solution)/shard_map/jrd,jrf->jdf/dot_general | solution.py:134
  279.0 3.8 %all-to-all-done.1 = bf16[8,96,1024]{2,1,0:T(8,128)(2,1)S(1)} async-done(((bf16[8,96,1024]{2,1,0:T(8,128)(2,1)}), bf16[8,96,1024]{2,1,0:T(8,128)(2,1)S(1)}, u32[]{:S(2)}, u32[]{:S(2)}) %all-to-all-start.1) | async-done | bytes 1572896 | tf_op jit(solution)/shard_map/all_to_all | solution.py:131
  282.8 2.1 gather_fusion.1
  (73 shorter events, 18.9 us)
Async XLA Ops:
  7.2 30.1 %all-gather.5.cloned.1.call-start = ((), (), s32[]{:S(2)}) async-start(), calls=%async_computation.4 | async-start | bytes 1216512 | tf_op jit(solution)/shard_map/all_gather | solution.py:49
  10.7 52.7 %all-gather.9.cloned.1.call-start = ((), (), s32[]{:S(2)}) async-start(), calls=%async_computation.7 | async-start | bytes 1216512 | tf_op jit(solution)/shard_map/all_gather | solution.py:57
  12.4 102.0 %reduce-scatter.3.cloned.1.call-start = ((), (), s32[]{:S(2)}) async-start(), calls=%async_computation.5 | async-start | bytes 2949120 | tf_op jit(solution)/shard_map/reduce_scatter | solution.py:96
  37.3 4.6 %copy-start.8 = (bf16[384,1408]{1,0:T(8,128)(2,1)S(1)}, bf16[384,1408]{1,0:T(8,128)(2,1)}, u32[]{:S(2)}) copy-start(bf16[384,1408]{1,0:T(8,128)(2,1)} %all-gather.5.cloned.1.call-done) | copy-start | bytes 3244036
  42.9 7.4 %copy-start.1 = (bf16[768,1024]{1,0:T(8,128)(2,1)}, bf16[768,1024]{1,0:T(8,128)(2,1)S(1)}, u32[]{:S(2)}) copy-start(bf16[768,1024]{1,0:T(8,128)(2,1)S(1)} %convolution_convert_fusion.3) | copy-start | bytes 4718596
  42.9 8.9 %copy-start = (bf16[8,1024,768]{2,1,0:T(8,128)(2,1)S(1)}, bf16[8,1024,768]{2,1,0:T(8,128)(2,1)}, u32[]{:S(2)}) copy-start(bf16[8,1024,768]{2,1,0:T(8,128)(2,1)} %param.13) | copy-start | bytes 37748740
  55.4 90.4 %reduce-scatter.5.cloned.1.call-start = ((), (), s32[]{:S(2)}) async-start(), calls=%async_computation.8 | async-start | bytes 1474560 | tf_op jit(solution)/shard_map/reduce_scatter | solution.py:100
  75.1 102.0 %all-gather.7.cloned.1.call-start = ((), (), s32[]{:S(2)}) async-start(), calls=%async_computation.6 | async-start | bytes 1474560 | tf_op jit(solution)/shard_map/all_gather | solution.py:107
  147.9 80.9 %all-gather.11.cloned.1.call-start = ((), (), s32[]{:S(2)}) async-start(), calls=%async_computation.9 | async-start | bytes 2949120 | tf_op jit(solution)/shard_map/all_gather | solution.py:108
  188.7 3.9 %copy-start.7 = (f32[48,8]{0,1:T(8,128)S(1)}, f32[48,8]{0,1:T(8,128)}, u32[]{:S(2)}) copy-start(f32[48,8]{0,1:T(8,128)} %param.12) | copy-start | bytes 4612
  188.7 4.0 %copy-start.6 = (s32[48,8]{0,1:T(8,128)S(1)}, s32[48,8]{0,1:T(8,128)}, u32[]{:S(2)}) copy-start(s32[48,8]{0,1:T(8,128)} %param.11) | copy-start | bytes 4612
  188.7 24.8 %all-to-all-start = ((bf16[8,96,1024]{2,1,0:T(8,128)(2,1)}), bf16[8,96,1024]{2,1,0:T(8,128)(2,1)S(1)}, u32[]{:S(2)}, u32[]{:S(2)}) async-start(bf16[8,96,1024]{2,1,0:T(8,128)(2,1)} %copy.63), calls=%async_computation.1 | async-start | bytes 3145728 | tf_op jit(solution)/shard_map/all_to_all | solution.py:121
  230.6 1.5 copy-start.3
  230.6 1.9 copy-start.5
  258.0 6.4 %copy-start.2 = (bf16[768,1024]{1,0:T(8,128)(2,1)S(1)}, bf16[768,1024]{1,0:T(8,128)(2,1)}, u32[]{:S(2)}) copy-start(bf16[768,1024]{1,0:T(8,128)(2,1)} %copy-done.1) | copy-start | bytes 4718596
  258.0 24.8 %all-to-all-start.1 = ((bf16[8,96,1024]{2,1,0:T(8,128)(2,1)}), bf16[8,96,1024]{2,1,0:T(8,128)(2,1)S(1)}, u32[]{:S(2)}, u32[]{:S(2)}) async-start(bf16[8,96,1024]{2,1,0:T(8,128)(2,1)} %copy.68), calls=%async_computation.3 | async-start | bytes 3145728 | tf_op jit(solution)/shard_map/all_to_all | solution.py:131
  264.4 8.0 %copy-start.4 = (bf16[768,768]{1,0:T(8,128)(2,1)S(1)}, bf16[768,768]{1,0:T(8,128)(2,1)}, u32[]{:S(2)}) copy-start(bf16[768,768]{1,0:T(8,128)(2,1)} %copy-done.3) | copy-start | bytes 3538948
Sparse Core Ops, SparseCore 0:
  10.9 26.3 all-gather.4
  39.7 23.6 all-gather.8
  66.3 48.0 reduce-scatter.2
  117.1 28.6 reduce-scatter.4
  148.0 29.1 all-gather.6
  179.2 49.5 all-gather.10

commit v4 on v2

--- a/solution.py
+++ b/solution.py
@@ -95,12 +95,17 @@
     back_part = jnp.einsum(
         "jrd,jfd->jrf", dy_in, down_weight, preferred_element_type=jnp.float32
     ).astype(jnp.bfloat16)
-    back_sums = lax.psum_scatter(
-        back_part.reshape(row_count, hidden_units), "dp", scatter_dimension=0, tiled=True
+    dp_count = lax.axis_size("dp")
+    back_blocks = lax.all_to_all(
+        back_part.reshape(row_count, hidden_units), "dp", split_axis=0, concat_axis=0, tiled=True
+    )
+    back_sums = jnp.sum(
+        back_blocks.reshape(dp_count, row_count // dp_count, hidden_units).astype(jnp.float32),
+        axis=0,
     )
     front_sums = front_sums.astype(jnp.float32)
     hidden, gate_delta, up_delta = swiglu_parts(
-        front_sums[:, :hidden_units], front_sums[:, hidden_units:], back_sums.astype(jnp.float32)
+        front_sums[:, :hidden_units], front_sums[:, hidden_units:], back_sums
     )
     hidden = lax.all_gather(hidden, "dp", axis=0, tiled=True)
     deltas = lax.all_gather(

time: 287 us -> 280 us (0.976)
  waiting for transfers between devices: 151 us -> 86.3 us
  blocking collectives: 0 us -> 59.3 us
    all_to_all x0 -> x1, blocking collectives: none -> 59.3 us  [local(): lax.all_to_all(back_part.reshape(row_count, hidden_units), 'dp', split_ax...]
    reduce_scatter x1, waiting for transfers between devices: 34.4 us -> 0.02 us  [local(): front_sums = lax.psum_scatter(front, 'dp', scatter_dimension=0, tiled=True)]
    reduce_scatter x1 -> x0, waiting for transfers between devices: 30.4 us -> none  [local(): lax.psum_scatter(back_part.reshape(row_count, hidden_units), 'dp', scatte...]
  transfers between devices with their start and end apart: 7 -> 6, of which waited for: 7 -> 5; matrix products, arithmetic and copies ran while one was open for 19% -> 19% of each run, Pallas kernels for 0% -> 0%
where the time goes in v4:
time: 280 us; the launch traced here: 279 us
  waiting for transfers between devices  86.3 us (31%)
  matrix products  63.4 us (23%)
  blocking collectives  59.3 us (21%)
  local copies, waits for them, and re-layouts  30 us (11%)
  other arithmetic  17.6 us (6%)
  between operations  14.1 us (5%)
  starting transfers between devices  8.25 us (3%)
    all_to_all x1, blocking collectives, local(): lax.all_to_all(back_part.reshape(row_count, hidden_units), 'dp', split_ax...  59.3 us
    all_gather x1, waiting for transfers between devices, local(): hidden = lax.all_gather(hidden, 'dp', axis=0, tiled=True)  28.9 us
    all_gather x1, waiting for transfers between devices, local(): gathered = lax.all_gather(packed, 'expert', axis=0, tiled=True)  28.8 us
    all_gather x1, waiting for transfers between devices, local(): lax.all_gather(jnp.concatenate([gate_delta, up_delta], axis=1), 'dp', axi...  12.6 us
    all_to_all x1, waiting for transfers between devices, local(): lax.all_to_all(expert_out.reshape(buffer_rows, width_dev), 'expert', spli...  12 us
    dot_general x1, matrix products, local(): jnp.einsum('jscf,jdf->sjcd', gate_delta, gate_weight, preferred_element_t...  10.6 us
    dot_general x1, matrix products, local(): jnp.einsum('jscf,jdf->sjcd', up_delta, up_weight, preferred_element_type=...  9.13 us
    dot_general x1, matrix products, local(): jnp.einsum('jrd,jfd->jrf', dy_in, down_weight, preferred_element_type=jnp...  9 us
  transfers between devices with their start and end apart: 6, of which 5 were waited for; matrix products, arithmetic and copies ran while one was open for 19% of the time, Pallas kernels for 0%

profile of v4, /device:TPU:0, one launch (start us, length us, event | category | flops | bytes accessed | tf_op | source)
XLA Modules:
  0.0 279.0 jit_solution(15859932520619938394)
XLA Ops:
  9.1 1.7 concatenate.9
  10.9 28.8 %all-gather.4.cloned.1.call-done = bf16[384,2176]{1,0:T(8,128)(2,1)} async-done(((bf16[48,2176]{1,0:T(8,128)(2,1)}), bf16[384,2176]{1,0:T(8,128)(2,1)}) %all-gather.4.cloned.1.call-update) | async-done | bytes 1671184 | tf_op jit(solution)/shard_map/all_gather | solution.py:52
  41.5 1.6 convert_reduce_fusion
  44.5 1.8 fusion.12
  46.3 3.2 %copy-done.3 = f32[768,2048]{1,0:T(8,128)} copy-done((f32[768,2048]{1,0:T(8,128)}, f32[768,2048]{1,0:T(8,128)S(1)}, u32[]{:S(2)}) %copy-start.3) | copy-done | bytes 6291480
  49.8 2.1 copy-done
  51.8 2.0 convolution_convert_fusion.4
  55.7 2.0 convolution_convert_fusion.5
  57.6 1.6 pad_maximum_fusion
  60.8 2.1 fusion.6
  63.0 9.0 %convolution_convert_fusion.3 = bf16[8,96,768]{2,1,0:T(8,128)(2,1)S(1)} fusion(bf16[8,96,1024]{2,1,0:T(8,128)(2,1)S(1)} %bitcast.65, bf16[8,768,1024]{2,1,0:T(8,128)(2,1)} %param.15), kind=kOutput, calls=%fused_computation.26 | convolution fusion | flops 1208549376 | bytes 15335424 | tf_op jit(solution)/shard_map/jrd,jfd->jrf/dot_general | solution.py:95
  72.0 59.3 %all_to_all.33 = bf16[4,192,768]{2,1,0:T(8,128)(2,1)S(1)} all-to-all(bf16[4,192,768]{2,1,0:T(8,128)(2,1)S(1)} %bitcast.72), channel_id=1, replica_groups=mesh['dp'=4,'expert'=8] {'dp'}, dimensions={0} | all-to-all | bytes 2359296 | tf_op jit(solution)/shard_map/all_to_all | solution.py:99
  134.7 28.9 %all-gather.6.cloned.1.call-done = bf16[768,768]{1,0:T(8,128)(2,1)} async-done(((bf16[192,768]{1,0:T(8,128)(2,1)}), bf16[768,768]{1,0:T(8,128)(2,1)}) %all-gather.6.cloned.1.call-update) | async-done | bytes 1179664 | tf_op jit(solution)/shard_map/all_gather | solution.py:110
  163.7 2.2 reshape.125
  165.8 6.4 %convert_bitcast_fusion = bf16[8,8,12,1024]{3,2,0,1:T(8,128)(2,1)S(1)} fusion(bf16[8,8,12,768]{3,2,1,0:T(8,128)(2,1)S(1)} %reshape.125, bf16[8,768,1024]{2,1,0:T(8,128)(2,1)} %param.15), kind=kOutput, calls=%fused_computation.22 | convolution fusion | flops 1208745984 | bytes 15335424 | tf_op jit(solution)/shard_map/jscf,jfd->sjcd/dot_general | solution.py:121
  173.1 2.0 copy.63
  175.1 3.9 %all-to-all-start = ((bf16[8,96,1024]{2,1,0:T(8,128)(2,1)}), bf16[8,96,1024]{2,1,0:T(8,128)(2,1)S(1)}, u32[]{:S(2)}, u32[]{:S(2)}) async-start(bf16[8,96,1024]{2,1,0:T(8,128)(2,1)} %copy.63), calls=%async_computation.1 | async-start | bytes 3145728 | tf_op jit(solution)/shard_map/all_to_all | solution.py:124
  180.1 7.9 %convolution_convert_fusion = bf16[8,768,1024]{2,1,0:T(8,128)(2,1)} fusion(bf16[8,96,768]{2,1,0:T(8,128)(2,1)} %bitcast.73, bf16[8,96,1024]{2,1,0:T(8,128)(2,1)S(1)} %bitcast.66), kind=kOutput, calls=%fused_computation.11 | convolution fusion | flops 1214251008 | bytes 15335424 | tf_op jit(solution)/shard_map/jrf,jrd->jfd/dot_general | solution.py:127
  187.9 12.0 %all-to-all-done = bf16[8,96,1024]{2,1,0:T(8,128)(2,1)S(1)} async-done(((bf16[8,96,1024]{2,1,0:T(8,128)(2,1)}), bf16[8,96,1024]{2,1,0:T(8,128)(2,1)S(1)}, u32[]{:S(2)}, u32[]{:S(2)}) %all-to-all-start) | async-done | bytes 1572896 | tf_op jit(solution)/shard_map/all_to_all | solution.py:124
  200.0 2.7 gather_fusion
  202.7 12.6 %all-gather.8.cloned.1.call-done = bf16[768,1536]{1,0:T(8,128)(2,1)} async-done(((bf16[192,1536]{1,0:T(8,128)(2,1)}), bf16[768,1536]{1,0:T(8,128)(2,1)}) %all-gather.8.cloned.1.call-update) | async-done | bytes 2359312 | tf_op jit(solution)/shard_map/all_gather | solution.py:111
  215.3 1.8 fusion.22
  220.3 9.1 %fusion = f32[8,8,12,1024]{3,2,1,0:T(8,128)S(1)} fusion(bf16[8,8,12,768]{3,2,1,0:T(8,128)(2,1)} %reshape.128, bf16[8,1024,768]{2,1,0:T(8,128)(2,1)} %param.14), kind=kOutput, calls=%fused_computation.2 | convolution fusion | flops 1207959552 | bytes 16908288 | tf_op jit(solution)/shard_map/jscf,jdf->sjcd/dot_general | solution.py:132
  229.4 10.6 %fusion.7 = bf16[8,8,12,1024]{3,2,0,1:T(8,128)(2,1)} fusion(f32[8,8,12,1024]{3,2,1,0:T(8,128)S(1)} %fusion, bf16[8,8,12,768]{3,2,1,0:T(8,128)(2,1)} %reshape.127, bf16[8,1024,768]{2,1,0:T(8,128)(2,1)} %param.13), kind=kOutput, calls=%fused_computation.21 | convolution fusion | flops 1209532416 | bytes 18481152 | tf_op jit(solution)/shard_map/jscf,jdf->sjcd/dot_general | solution.py:131
  240.0 2.5 copy.67
  242.5 2.0 copy.68
  244.5 4.0 %all-to-all-start.2 = ((bf16[8,96,1024]{2,1,0:T(8,128)(2,1)}), bf16[8,96,1024]{2,1,0:T(8,128)(2,1)S(1)}, u32[]{:S(2)}, u32[]{:S(2)}) async-start(bf16[8,96,1024]{2,1,0:T(8,128)(2,1)} %copy.68), calls=%async_computation.3 | async-start | bytes 3145728 | tf_op jit(solution)/shard_map/all_to_all | solution.py:134
  248.5 2.4 multiply_reduce_fusion
  250.9 8.0 %convolution_convert_fusion.1 = bf16[8,1024,768]{2,1,0:T(8,128)(2,1)} fusion(bf16[8,96,1024]{2,1,0:T(8,128)(2,1)S(1)} %bitcast.61, bf16[8,96,768]{2,1,0:T(8,128)(2,1)} %bitcast.68), kind=kOutput, calls=%fused_computation.12 | convolution fusion | flops 1214251008 | bytes 15335424 | tf_op jit(solution)/shard_map/jrd,jrf->jdf/dot_general | solution.py:140
  258.9 6.6 %convolution_convert_fusion.2 = bf16[8,1024,768]{2,1,0:T(8,128)(2,1)} fusion(bf16[8,96,1024]{2,1,0:T(8,128)(2,1)S(1)} %bitcast.62, bf16[8,96,768]{2,1,0:T(8,128)(2,1)S(1)} %bitcast.67), kind=kOutput, calls=%fused_computation.13 | convolution fusion | flops 1214251008 | bytes 15335424 | tf_op jit(solution)/shard_map/jrd,jrf->jdf/dot_general | solution.py:137
  265.5 3.8 %all-to-all-done.2 = bf16[8,96,1024]{2,1,0:T(8,128)(2,1)S(1)} async-done(((bf16[8,96,1024]{2,1,0:T(8,128)(2,1)}), bf16[8,96,1024]{2,1,0:T(8,128)(2,1)S(1)}, u32[]{:S(2)}, u32[]{:S(2)}) %all-to-all-start.2) | async-done | bytes 1572896 | tf_op jit(solution)/shard_map/all_to_all | solution.py:134
  269.3 2.1 gather_fusion.1
  (77 shorter events, 18.1 us)
Async XLA Ops:
  7.2 32.6 %all-gather.4.cloned.1.call-start = ((), (), s32[]{:S(2)}) async-start(), calls=%async_computation.4 | async-start | bytes 1880064 | tf_op jit(solution)/shard_map/all_gather | solution.py:52
  10.8 120.7 %reduce-scatter.2.cloned.1.call-start = ((), (), s32[]{:S(2)}) async-start(), calls=%async_computation.5 | async-start | bytes 2949120 | tf_op jit(solution)/shard_map/reduce_scatter | solution.py:94
  39.8 4.7 %copy-start.7 = (bf16[384,2176]{1,0:T(8,128)(2,1)S(1)}, bf16[384,2176]{1,0:T(8,128)(2,1)}, u32[]{:S(2)}) copy-start(bf16[384,2176]{1,0:T(8,128)(2,1)} %all-gather.4.cloned.1.call-done) | copy-start | bytes 5013508
  44.4 7.4 %copy-start = (bf16[8,1024,768]{2,1,0:T(8,128)(2,1)S(1)}, bf16[8,1024,768]{2,1,0:T(8,128)(2,1)}, u32[]{:S(2)}) copy-start(bf16[8,1024,768]{2,1,0:T(8,128)(2,1)} %param.14) | copy-start | bytes 37748740
  44.4 9.4 %slice-start = ((s8[12582912]{0:T(1024)(128)(4,1)}), s8[4194304]{0:T(1024)(128)(4,1)S(1)}, s32[]{:S(2)}) async-start(s8[12582912]{0:T(1024)(128)(4,1)} %bitcast.57), calls=%async_computation.8 | async-start | bytes 8388608
  44.5 9.8 %slice-start.1 = ((s8[12582912]{0:T(1024)(128)(4,1)}), s8[4194304]{0:T(1024)(128)(4,1)S(1)}, s32[]{:S(2)}) async-start(s8[12582912]{0:T(1024)(128)(4,1)} %bitcast.57), calls=%async_computation.9 | async-start | bytes 8388608
  46.3 3.2 %copy-start.3 = (f32[768,2048]{1,0:T(8,128)}, f32[768,2048]{1,0:T(8,128)S(1)}, u32[]{:S(2)}) copy-start(f32[768,2048]{1,0:T(8,128)S(1)} %fusion.12) | copy-start | bytes 18874372
  49.8 4.1 %copy-start.1 = (bf16[768,1024]{1,0:T(8,128)(2,1)}, bf16[768,1024]{1,0:T(8,128)(2,1)S(1)}, u32[]{:S(2)}) copy-start(bf16[768,1024]{1,0:T(8,128)(2,1)S(1)} %slice.90) | copy-start | bytes 4718596
  51.8 3.8 %slice-start.2 = ((s8[12582912]{0:T(1024)(128)(4,1)}), s8[4194304]{0:T(1024)(128)(4,1)S(1)}, s32[]{:S(2)}) async-start(s8[12582912]{0:T(1024)(128)(4,1)} %bitcast.57), calls=%async_computation.10 | async-start | bytes 8388608
  59.3 104.4 %all-gather.6.cloned.1.call-start = ((), (), s32[]{:S(2)}) async-start(), calls=%async_computation.6 | async-start | bytes 1474560 | tf_op jit(solution)/shard_map/all_gather | solution.py:110
  133.8 81.5 %all-gather.8.cloned.1.call-start = ((), (), s32[]{:S(2)}) async-start(), calls=%async_computation.7 | async-start | bytes 2949120 | tf_op jit(solution)/shard_map/all_gather | solution.py:111
  175.1 3.9 %copy-start.9 = (f32[48,8]{0,1:T(8,128)S(1)}, f32[48,8]{0,1:T(8,128)}, u32[]{:S(2)}) copy-start(f32[48,8]{0,1:T(8,128)} %param.12) | copy-start | bytes 4612
  175.1 4.0 %copy-start.8 = (s32[48,8]{0,1:T(8,128)S(1)}, s32[48,8]{0,1:T(8,128)}, u32[]{:S(2)}) copy-start(s32[48,8]{0,1:T(8,128)} %param.11) | copy-start | bytes 4612
  175.1 24.8 %all-to-all-start = ((bf16[8,96,1024]{2,1,0:T(8,128)(2,1)}), bf16[8,96,1024]{2,1,0:T(8,128)(2,1)S(1)}, u32[]{:S(2)}, u32[]{:S(2)}) async-start(bf16[8,96,1024]{2,1,0:T(8,128)(2,1)} %copy.63), calls=%async_computation.1 | async-start | bytes 3145728 | tf_op jit(solution)/shard_map/all_to_all | solution.py:124
  217.1 1.5 copy-start.4
  217.1 1.9 copy-start.6
  244.5 6.4 %copy-start.2 = (bf16[768,1024]{1,0:T(8,128)(2,1)S(1)}, bf16[768,1024]{1,0:T(8,128)(2,1)}, u32[]{:S(2)}) copy-start(bf16[768,1024]{1,0:T(8,128)(2,1)} %copy-done.1) | copy-start | bytes 4718596
  244.5 24.8 %all-to-all-start.2 = ((bf16[8,96,1024]{2,1,0:T(8,128)(2,1)}), bf16[8,96,1024]{2,1,0:T(8,128)(2,1)S(1)}, u32[]{:S(2)}, u32[]{:S(2)}) async-start(bf16[8,96,1024]{2,1,0:T(8,128)(2,1)} %copy.68), calls=%async_computation.3 | async-start | bytes 3145728 | tf_op jit(solution)/shard_map/all_to_all | solution.py:134
  250.9 8.0 %copy-start.5 = (bf16[768,768]{1,0:T(8,128)(2,1)S(1)}, bf16[768,768]{1,0:T(8,128)(2,1)}, u32[]{:S(2)}) copy-start(bf16[768,768]{1,0:T(8,128)(2,1)} %copy-done.4) | copy-start | bytes 3538948
Sparse Core Ops, SparseCore 0:
  10.9 28.7 all-gather.3
  59.4 66.6 reduce-scatter.1
  133.9 29.7 all-gather.5
  165.7 49.5 all-gather.7

commit v5 on v4

--- a/solution.py
+++ b/solution.py
@@ -107,9 +107,17 @@
     hidden, gate_delta, up_delta = swiglu_parts(
         front_sums[:, :hidden_units], front_sums[:, hidden_units:], back_sums
     )
-    hidden = lax.all_gather(hidden, "dp", axis=0, tiled=True)
     deltas = lax.all_gather(
         jnp.concatenate([gate_delta, up_delta], axis=1), "dp", axis=0, tiled=True
+    )
+    hidden = lax.all_to_all(
+        jnp.broadcast_to(hidden[None], (dp_count,) + hidden.shape).reshape(
+            dp_count * hidden.shape[0], hidden_units
+        ),
+        "dp",
+        split_axis=0,
+        concat_axis=0,
+        tiled=True,
     )
     expert_shape = (local_experts, sources, capacity, hidden_units)
     hidden = hidden.reshape(expert_shape)

time: 280 us -> 290 us (1.036)
  waiting for transfers between devices: 86.3 us -> 93.5 us
  starting transfers between devices: 8.25 us -> 11.3 us
    all_to_all x0 -> x1, waiting for transfers between devices: none -> 48.8 us  [local(): lax.all_to_all(jnp.broadcast_to(hidden[None], (dp_count,) + hidden.shape)...]
    all_gather x1 -> x0, waiting for transfers between devices: 28.9 us -> none  [local(): hidden = lax.all_gather(hidden, 'dp', axis=0, tiled=True)]
    all_gather x1, waiting for transfers between devices: 12.6 us -> 0.01 us  [local(): lax.all_gather(jnp.concatenate([gate_delta, up_delta], axis=1), 'dp', axi...]
    all_to_all x0 -> x1, starting transfers between devices: none -> 3.53 us  [local(): lax.all_to_all(jnp.broadcast_to(hidden[None], (dp_count,) + hidden.shape)...]
    unnamed x28 -> x30, local copies, waits for them, and re-layouts: 7.75 us -> 7.75 us
  transfers between devices with their start and end apart: 6 -> 6, of which waited for: 5 -> 4; matrix products, arithmetic and copies ran while one was open for 19% -> 18% of each run, Pallas kernels for 0% -> 0%
where the time goes in v5:
time: 290 us; the launch traced here: 289 us
  waiting for transfers between devices  93.5 us (32%)
  matrix products  63.9 us (22%)
  blocking collectives  59.5 us (21%)
  local copies, waits for them, and re-layouts  30.2 us (10%)
  other arithmetic  16.9 us (6%)
  between operations  14.1 us (5%)
  starting transfers between devices  11.3 us (4%)
    all_to_all x1, blocking collectives, local(): lax.all_to_all(back_part.reshape(row_count, hidden_units), 'dp', split_ax...  59.5 us
    all_to_all x1, waiting for transfers between devices, local(): lax.all_to_all(jnp.broadcast_to(hidden[None], (dp_count,) + hidden.shape)...  48.8 us
    all_gather x1, waiting for transfers between devices, local(): gathered = lax.all_gather(packed, 'expert', axis=0, tiled=True)  28.8 us
    all_to_all x1, waiting for transfers between devices, local(): lax.all_to_all(expert_out.reshape(buffer_rows, width_dev), 'expert', spli...  12.1 us
    dot_general x1, matrix products, local(): jnp.einsum('jscf,jdf->sjcd', gate_delta, gate_weight, preferred_element_t...  10.6 us
    dot_general x1, matrix products, local(): jnp.einsum('jscf,jdf->sjcd', up_delta, up_weight, preferred_element_type=...  9.11 us
    dot_general x1, matrix products, local(): jnp.einsum('jrd,jfd->jrf', dy_in, down_weight, preferred_element_type=jnp...  9 us
    dot_general x1, matrix products, local(): jnp.einsum('jrd,jrf->jdf', x_in, up_delta.reshape(rows_shape), preferred_...  7.99 us
  transfers between devices with their start and end apart: 6, of which 4 were waited for; matrix products, arithmetic and copies ran while one was open for 18% of the time, Pallas kernels for 0%

profile of v5, /device:TPU:0, one launch (start us, length us, event | category | flops | bytes accessed | tf_op | source)
XLA Modules:
  0.0 289.5 jit_solution(9840163775606186787)
XLA Ops:
  9.1 1.7 concatenate.9
  10.9 28.8 %all-gather.3.cloned.1.call-done = bf16[384,2176]{1,0:T(8,128)(2,1)} async-done(((bf16[48,2176]{1,0:T(8,128)(2,1)}), bf16[384,2176]{1,0:T(8,128)(2,1)}) %all-gather.3.cloned.1.call-update) | async-done | bytes 1671184 | tf_op jit(solution)/shard_map/all_gather | solution.py:52
  41.5 1.6 convert_reduce_fusion
  44.5 1.8 fusion.12
  46.3 3.2 %copy-done.3 = f32[768,2048]{1,0:T(8,128)} copy-done((f32[768,2048]{1,0:T(8,128)}, f32[768,2048]{1,0:T(8,128)S(1)}, u32[]{:S(2)}) %copy-start.3) | copy-done | bytes 6291480
  49.8 2.1 copy-done
  51.8 2.0 convolution_convert_fusion.4
  55.7 2.0 convolution_convert_fusion.5
  57.6 1.6 pad_maximum_fusion
  60.6 2.1 fusion.6
  62.7 9.0 %convolution_convert_fusion.3 = bf16[8,96,768]{2,1,0:T(8,128)(2,1)S(1)} fusion(bf16[8,96,1024]{2,1,0:T(8,128)(2,1)S(1)} %bitcast.65, bf16[8,768,1024]{2,1,0:T(8,128)(2,1)} %param.15), kind=kOutput, calls=%fused_computation.26 | convolution fusion | flops 1208549376 | bytes 15335424 | tf_op jit(solution)/shard_map/jrd,jfd->jrf/dot_general | solution.py:95
  71.7 59.5 %all_to_all.39 = bf16[4,192,768]{2,1,0:T(8,128)(2,1)S(1)} all-to-all(bf16[4,192,768]{2,1,0:T(8,128)(2,1)S(1)} %bitcast.73), channel_id=1, replica_groups=mesh['dp'=4,'expert'=8] {'dp'}, dimensions={0} | all-to-all | bytes 2359296 | tf_op jit(solution)/shard_map/all_to_all | solution.py:99
  134.0 3.5 %all-to-all-start = ((bf16[4,192,768]{2,1,0:T(8,128)(2,1)}), bf16[4,192,768]{2,1,0:T(8,128)(2,1)S(1)}, u32[]{:S(2)}, u32[]{:S(2)}) async-start(bf16[4,192,768]{2,1,0:T(8,128)(2,1)} %broadcast_in_dim.63), calls=%async_computation.1 | async-start | bytes 2359296 | tf_op jit(solution)/shard_map/all_to_all | solution.py:113
  138.5 48.8 %all-to-all-done = bf16[4,192,768]{2,1,0:T(8,128)(2,1)S(1)} async-done(((bf16[4,192,768]{2,1,0:T(8,128)(2,1)}), bf16[4,192,768]{2,1,0:T(8,128)(2,1)S(1)}, u32[]{:S(2)}, u32[]{:S(2)}) %all-to-all-start) | async-done | bytes 1179680 | tf_op jit(solution)/shard_map/all_to_all | solution.py:113
  188.7 6.9 %convert_bitcast_fusion = bf16[8,8,12,1024]{3,2,0,1:T(8,128)(2,1)S(1)} fusion(bf16[8,8,12,768]{3,2,1,0:T(8,128)(2,1)} %reshape.132, bf16[8,768,1024]{2,1,0:T(8,128)(2,1)} %param.15), kind=kOutput, calls=%fused_computation.22 | convolution fusion | flops 1208745984 | bytes 15335424 | tf_op jit(solution)/shard_map/jscf,jfd->sjcd/dot_general | solution.py:129
  196.6 2.0 copy.63
  198.6 3.7 %all-to-all-start.1 = ((bf16[8,96,1024]{2,1,0:T(8,128)(2,1)}), bf16[8,96,1024]{2,1,0:T(8,128)(2,1)S(1)}, u32[]{:S(2)}, u32[]{:S(2)}) async-start(bf16[8,96,1024]{2,1,0:T(8,128)(2,1)} %copy.63), calls=%async_computation.2 | async-start | bytes 3145728 | tf_op jit(solution)/shard_map/all_to_all | solution.py:132
  203.3 7.9 %convolution_convert_fusion = bf16[8,768,1024]{2,1,0:T(8,128)(2,1)} fusion(bf16[8,96,768]{2,1,0:T(8,128)(2,1)} %bitcast.67, bf16[8,96,1024]{2,1,0:T(8,128)(2,1)S(1)} %bitcast.66), kind=kOutput, calls=%fused_computation.11 | convolution fusion | flops 1214251008 | bytes 15335424 | tf_op jit(solution)/shard_map/jrf,jrd->jfd/dot_general | solution.py:135
  211.2 12.1 %all-to-all-done.1 = bf16[8,96,1024]{2,1,0:T(8,128)(2,1)S(1)} async-done(((bf16[8,96,1024]{2,1,0:T(8,128)(2,1)}), bf16[8,96,1024]{2,1,0:T(8,128)(2,1)S(1)}, u32[]{:S(2)}, u32[]{:S(2)}) %all-to-all-start.1) | async-done | bytes 1572896 | tf_op jit(solution)/shard_map/all_to_all | solution.py:132
  223.3 2.7 gather_fusion
  225.9 1.8 fusion.22
  227.7 1.4 reshape.134
  230.9 9.1 %fusion = f32[8,8,12,1024]{3,2,1,0:T(8,128)S(1)} fusion(bf16[8,8,12,768]{3,2,1,0:T(8,128)(2,1)} %reshape.135, bf16[8,1024,768]{2,1,0:T(8,128)(2,1)} %param.14), kind=kOutput, calls=%fused_computation.2 | convolution fusion | flops 1207959552 | bytes 16908288 | tf_op jit(solution)/shard_map/jscf,jdf->sjcd/dot_general | solution.py:140
  240.0 10.6 %fusion.7 = bf16[8,8,12,1024]{3,2,0,1:T(8,128)(2,1)} fusion(f32[8,8,12,1024]{3,2,1,0:T(8,128)S(1)} %fusion, bf16[8,8,12,768]{3,2,1,0:T(8,128)(2,1)} %reshape.134, bf16[8,1024,768]{2,1,0:T(8,128)(2,1)} %param.13), kind=kOutput, calls=%fused_computation.21 | convolution fusion | flops 1209532416 | bytes 18481152 | tf_op jit(solution)/shard_map/jscf,jdf->sjcd/dot_general | solution.py:139
  250.6 2.5 copy.67
  253.1 2.0 copy.68
  255.1 3.9 %all-to-all-start.3 = ((bf16[8,96,1024]{2,1,0:T(8,128)(2,1)}), bf16[8,96,1024]{2,1,0:T(8,128)(2,1)S(1)}, u32[]{:S(2)}, u32[]{:S(2)}) async-start(bf16[8,96,1024]{2,1,0:T(8,128)(2,1)} %copy.68), calls=%async_computation.4 | async-start | bytes 3145728 | tf_op jit(solution)/shard_map/all_to_all | solution.py:142
  259.0 2.4 multiply_reduce_fusion
  261.5 8.0 %convolution_convert_fusion.1 = bf16[8,1024,768]{2,1,0:T(8,128)(2,1)} fusion(bf16[8,96,1024]{2,1,0:T(8,128)(2,1)S(1)} %bitcast.61, bf16[8,96,768]{2,1,0:T(8,128)(2,1)} %bitcast.69), kind=kOutput, calls=%fused_computation.12 | convolution fusion | flops 1214251008 | bytes 15335424 | tf_op jit(solution)/shard_map/jrd,jrf->jdf/dot_general | solution.py:148
  269.5 6.6 %convolution_convert_fusion.2 = bf16[8,1024,768]{2,1,0:T(8,128)(2,1)} fusion(bf16[8,96,1024]{2,1,0:T(8,128)(2,1)S(1)} %bitcast.62, bf16[8,96,768]{2,1,0:T(8,128)(2,1)S(1)} %bitcast.68), kind=kOutput, calls=%fused_computation.13 | convolution fusion | flops 1214251008 | bytes 15335424 | tf_op jit(solution)/shard_map/jrd,jrf->jdf/dot_general | solution.py:145
  276.1 3.7 %all-to-all-done.3 = bf16[8,96,1024]{2,1,0:T(8,128)(2,1)S(1)} async-done(((bf16[8,96,1024]{2,1,0:T(8,128)(2,1)}), bf16[8,96,1024]{2,1,0:T(8,128)(2,1)S(1)}, u32[]{:S(2)}, u32[]{:S(2)}) %all-to-all-start.3) | async-done | bytes 1572896 | tf_op jit(solution)/shard_map/all_to_all | solution.py:142
  279.8 2.1 gather_fusion.1
  (79 shorter events, 18.2 us)
Async XLA Ops:
  7.2 32.6 %all-gather.3.cloned.1.call-start = ((), (), s32[]{:S(2)}) async-start(), calls=%async_computation.5 | async-start | bytes 1880064 | tf_op jit(solution)/shard_map/all_gather | solution.py:52
  10.8 120.6 %reduce-scatter.2.cloned.1.call-start = ((), (), s32[]{:S(2)}) async-start(), calls=%async_computation.6 | async-start | bytes 2949120 | tf_op jit(solution)/shard_map/reduce_scatter | solution.py:94
  39.8 4.7 %copy-start.8 = (bf16[384,2176]{1,0:T(8,128)(2,1)S(1)}, bf16[384,2176]{1,0:T(8,128)(2,1)}, u32[]{:S(2)}) copy-start(bf16[384,2176]{1,0:T(8,128)(2,1)} %all-gather.3.cloned.1.call-done) | copy-start | bytes 5013508
  44.4 7.4 %copy-start = (bf16[8,1024,768]{2,1,0:T(8,128)(2,1)S(1)}, bf16[8,1024,768]{2,1,0:T(8,128)(2,1)}, u32[]{:S(2)}) copy-start(bf16[8,1024,768]{2,1,0:T(8,128)(2,1)} %param.14) | copy-start | bytes 37748740
  44.4 9.4 %slice-start = ((s8[12582912]{0:T(1024)(128)(4,1)}), s8[4194304]{0:T(1024)(128)(4,1)S(1)}, s32[]{:S(2)}) async-start(s8[12582912]{0:T(1024)(128)(4,1)} %bitcast.57), calls=%async_computation.8 | async-start | bytes 8388608
  44.5 9.8 %slice-start.1 = ((s8[12582912]{0:T(1024)(128)(4,1)}), s8[4194304]{0:T(1024)(128)(4,1)S(1)}, s32[]{:S(2)}) async-start(s8[12582912]{0:T(1024)(128)(4,1)} %bitcast.57), calls=%async_computation.9 | async-start | bytes 8388608
  46.3 3.2 %copy-start.3 = (f32[768,2048]{1,0:T(8,128)}, f32[768,2048]{1,0:T(8,128)S(1)}, u32[]{:S(2)}) copy-start(f32[768,2048]{1,0:T(8,128)S(1)} %fusion.12) | copy-start | bytes 18874372
  49.8 4.1 %copy-start.1 = (bf16[768,1024]{1,0:T(8,128)(2,1)}, bf16[768,1024]{1,0:T(8,128)(2,1)S(1)}, u32[]{:S(2)}) copy-start(bf16[768,1024]{1,0:T(8,128)(2,1)S(1)} %slice.90) | copy-start | bytes 4718596
  51.8 3.8 %slice-start.2 = ((s8[12582912]{0:T(1024)(128)(4,1)}), s8[4194304]{0:T(1024)(128)(4,1)S(1)}, s32[]{:S(2)}) async-start(s8[12582912]{0:T(1024)(128)(4,1)} %bitcast.57), calls=%async_computation.10 | async-start | bytes 8388608
  134.0 53.3 %all-to-all-start = ((bf16[4,192,768]{2,1,0:T(8,128)(2,1)}), bf16[4,192,768]{2,1,0:T(8,128)(2,1)S(1)}, u32[]{:S(2)}, u32[]{:S(2)}) async-start(bf16[4,192,768]{2,1,0:T(8,128)(2,1)} %broadcast_in_dim.63), calls=%async_computation.1 | async-start | bytes 2359296 | tf_op jit(solution)/shard_map/all_to_all | solution.py:113
  137.6 88.3 %all-gather.5.cloned.1.call-start = ((), (), s32[]{:S(2)}) async-start(), calls=%async_computation.7 | async-start | bytes 2949120 | tf_op jit(solution)/shard_map/all_gather | solution.py:110
  187.3 8.3 %copy-start.4 = (bf16[4,192,768]{2,1,0:T(8,128)(2,1)}, bf16[4,192,768]{2,1,0:T(8,128)(2,1)S(1)}, u32[]{:S(2)}) copy-start(bf16[4,192,768]{2,1,0:T(8,128)(2,1)S(1)} %all-to-all-done) | copy-start | bytes 3538948
  198.6 3.7 %copy-start.10 = (f32[48,8]{0,1:T(8,128)S(1)}, f32[48,8]{0,1:T(8,128)}, u32[]{:S(2)}) copy-start(f32[48,8]{0,1:T(8,128)} %param.12) | copy-start | bytes 4612
  198.6 3.8 %copy-start.9 = (s32[48,8]{0,1:T(8,128)S(1)}, s32[48,8]{0,1:T(8,128)}, u32[]{:S(2)}) copy-start(s32[48,8]{0,1:T(8,128)} %param.11) | copy-start | bytes 4612
  198.6 24.7 %all-to-all-start.1 = ((bf16[8,96,1024]{2,1,0:T(8,128)(2,1)}), bf16[8,96,1024]{2,1,0:T(8,128)(2,1)S(1)}, u32[]{:S(2)}, u32[]{:S(2)}) async-start(bf16[8,96,1024]{2,1,0:T(8,128)(2,1)} %copy.63), calls=%async_computation.2 | async-start | bytes 3145728 | tf_op jit(solution)/shard_map/all_to_all | solution.py:132
  227.7 1.5 copy-start.5
  227.7 1.9 copy-start.7
  255.1 6.4 %copy-start.2 = (bf16[768,1024]{1,0:T(8,128)(2,1)S(1)}, bf16[768,1024]{1,0:T(8,128)(2,1)}, u32[]{:S(2)}) copy-start(bf16[768,1024]{1,0:T(8,128)(2,1)} %copy-done.1) | copy-start | bytes 4718596
  255.1 24.7 %all-to-all-start.3 = ((bf16[8,96,1024]{2,1,0:T(8,128)(2,1)}), bf16[8,96,1024]{2,1,0:T(8,128)(2,1)S(1)}, u32[]{:S(2)}, u32[]{:S(2)}) async-start(bf16[8,96,1024]{2,1,0:T(8,128)(2,1)} %copy.68), calls=%async_computation.4 | async-start | bytes 3145728 | tf_op jit(solution)/shard_map/all_to_all | solution.py:142
  261.5 8.0 %copy-start.6 = (bf16[768,768]{1,0:T(8,128)(2,1)S(1)}, bf16[768,768]{1,0:T(8,128)(2,1)}, u32[]{:S(2)}) copy-start(bf16[768,768]{1,0:T(8,128)(2,1)} %copy-done.5) | copy-start | bytes 3538948
Sparse Core Ops, SparseCore 0:
  10.9 28.7 all-gather.2
  59.4 66.7 reduce-scatter.1
  140.0 64.7 all-gather.4

commit v6 on v4

--- a/solution.py
+++ b/solution.py
@@ -49,7 +49,15 @@
         ],
         axis=1,
     )
-    gathered = lax.all_gather(packed, "expert", axis=0, tiled=True)
+    gathered = lax.all_to_all(
+        jnp.broadcast_to(packed[None], (sources,) + packed.shape).reshape(
+            sources * token_count, packed.shape[1]
+        ),
+        "expert",
+        split_axis=0,
+        concat_axis=0,
+        tiled=True,
+    )
     feats = gathered[:, : 2 * width_dev]
     route_all = gathered[:, 2 * width_dev : 2 * width_dev + route_cols].astype(jnp.float32)
     ids_all = route_all[:, :per_token].astype(jnp.int32)

time: 280 us -> 277 us (0.989)
  waiting for transfers between devices: 86.3 us -> 80 us
  starting transfers between devices: 8.25 us -> 13.4 us
    all_gather x1 -> x0, waiting for transfers between devices: 28.8 us -> none  [local(): gathered = lax.all_gather(packed, 'expert', axis=0, tiled=True)]
    all_to_all x0 -> x1, waiting for transfers between devices: none -> 22 us  [local(): lax.all_to_all(jnp.broadcast_to(packed[None], (sources,) + packed.shape)....]
    all_to_all x0 -> x1, starting transfers between devices: none -> 5.17 us  [local(): lax.all_to_all(jnp.broadcast_to(packed[None], (sources,) + packed.shape)....]
    unnamed x28 -> x26, local copies, waits for them, and re-layouts: 7.75 us -> 7.73 us
where the time goes in v6:
time: 277 us; the launch traced here: 276 us
  waiting for transfers between devices  80 us (29%)
  matrix products  63.4 us (23%)
  blocking collectives  58.3 us (21%)
  local copies, waits for them, and re-layouts  30.6 us (11%)
  other arithmetic  16.6 us (6%)
  between operations  14.1 us (5%)
  starting transfers between devices  13.4 us (5%)
    all_to_all x1, blocking collectives, local(): lax.all_to_all(back_part.reshape(row_count, hidden_units), 'dp', split_ax...  58.3 us
    all_gather x1, waiting for transfers between devices, local(): hidden = lax.all_gather(hidden, 'dp', axis=0, tiled=True)  29.4 us
    all_to_all x1, waiting for transfers between devices, local(): lax.all_to_all(jnp.broadcast_to(packed[None], (sources,) + packed.shape)....  22 us
    all_gather x1, waiting for transfers between devices, local(): lax.all_gather(jnp.concatenate([gate_delta, up_delta], axis=1), 'dp', axi...  12.8 us
    all_to_all x1, waiting for transfers between devices, local(): lax.all_to_all(expert_out.reshape(buffer_rows, width_dev), 'expert', spli...  12 us
    dot_general x1, matrix products, local(): jnp.einsum('jscf,jdf->sjcd', gate_delta, gate_weight, preferred_element_t...  10.6 us
    dot_general x1, matrix products, local(): jnp.einsum('jscf,jdf->sjcd', up_delta, up_weight, preferred_element_type=...  9.14 us
    dot_general x1, matrix products, local(): jnp.einsum('jrd,jfd->jrf', dy_in, down_weight, preferred_element_type=jnp...  9 us
  transfers between devices with their start and end apart: 6, of which 5 were waited for; matrix products, arithmetic and copies ran while one was open for 19% of the time, Pallas kernels for 0%

profile of v6, /device:TPU:0, one launch (start us, length us, event | category | flops | bytes accessed | tf_op | source)
XLA Modules:
  0.0 276.3 jit_solution(11557150615398107538)
XLA Ops:
  11.3 5.2 %all-to-all-start = ((bf16[8,48,2176]{2,1,0:T(8,128)(2,1)}), bf16[8,48,2176]{2,1,0:T(8,128)(2,1)S(1)}, u32[]{:S(2)}, u32[]{:S(2)}) async-start(bf16[8,48,2176]{2,1,0:T(8,128)(2,1)} %broadcast_in_dim.60), calls=%async_computation | async-start | bytes 3342336 | tf_op jit(solution)/shard_map/all_to_all | solution.py:52
  16.6 22.0 %all-to-all-done = bf16[8,48,2176]{2,1,0:T(8,128)(2,1)S(1)} async-done(((bf16[8,48,2176]{2,1,0:T(8,128)(2,1)}), bf16[8,48,2176]{2,1,0:T(8,128)(2,1)S(1)}, u32[]{:S(2)}, u32[]{:S(2)}) %all-to-all-start) | async-done | bytes 1671200 | tf_op jit(solution)/shard_map/all_to_all | solution.py:52
  39.4 1.6 convert_reduce_fusion
  42.3 1.8 fusion.12
  44.1 3.2 %copy-done.3 = f32[768,2048]{1,0:T(8,128)} copy-done((f32[768,2048]{1,0:T(8,128)}, f32[768,2048]{1,0:T(8,128)S(1)}, u32[]{:S(2)}) %copy-start.3) | copy-done | bytes 6291480
  47.6 2.1 copy-done
  49.7 2.0 convolution_convert_fusion.4
  53.5 2.0 convolution_convert_fusion.5
  55.5 1.6 pad_maximum_fusion
  58.7 2.1 fusion.6
  60.8 9.0 %convolution_convert_fusion.3 = bf16[8,96,768]{2,1,0:T(8,128)(2,1)S(1)} fusion(bf16[8,96,1024]{2,1,0:T(8,128)(2,1)S(1)} %bitcast.66, bf16[8,768,1024]{2,1,0:T(8,128)(2,1)} %param.15), kind=kOutput, calls=%fused_computation.26 | convolution fusion | flops 1208549376 | bytes 15335424 | tf_op jit(solution)/shard_map/jrd,jfd->jrf/dot_general | solution.py:103
  69.8 58.3 %all_to_all.42 = bf16[4,192,768]{2,1,0:T(8,128)(2,1)S(1)} all-to-all(bf16[4,192,768]{2,1,0:T(8,128)(2,1)S(1)} %bitcast.75), channel_id=1, replica_groups=mesh['dp'=4,'expert'=8] {'dp'}, dimensions={0} | all-to-all | bytes 2359296 | tf_op jit(solution)/shard_map/all_to_all | solution.py:107
  131.5 29.4 %all-gather.3.cloned.1.call-done = bf16[768,768]{1,0:T(8,128)(2,1)} async-done(((bf16[192,768]{1,0:T(8,128)(2,1)}), bf16[768,768]{1,0:T(8,128)(2,1)}) %all-gather.3.cloned.1.call-update) | async-done | bytes 1179664 | tf_op jit(solution)/shard_map/all_gather | solution.py:118
  160.9 2.2 reshape.130
  163.1 6.4 %convert_bitcast_fusion = bf16[8,8,12,1024]{3,2,0,1:T(8,128)(2,1)S(1)} fusion(bf16[8,8,12,768]{3,2,1,0:T(8,128)(2,1)S(1)} %reshape.130, bf16[8,768,1024]{2,1,0:T(8,128)(2,1)} %param.15), kind=kOutput, calls=%fused_computation.22 | convolution fusion | flops 1208745984 | bytes 15335424 | tf_op jit(solution)/shard_map/jscf,jfd->sjcd/dot_general | solution.py:129
  170.4 2.0 copy.63
  172.4 3.9 %all-to-all-start.1 = ((bf16[8,96,1024]{2,1,0:T(8,128)(2,1)}), bf16[8,96,1024]{2,1,0:T(8,128)(2,1)S(1)}, u32[]{:S(2)}, u32[]{:S(2)}) async-start(bf16[8,96,1024]{2,1,0:T(8,128)(2,1)} %copy.63), calls=%async_computation.2 | async-start | bytes 3145728 | tf_op jit(solution)/shard_map/all_to_all | solution.py:132
  177.3 7.9 %convolution_convert_fusion = bf16[8,768,1024]{2,1,0:T(8,128)(2,1)} fusion(bf16[8,96,768]{2,1,0:T(8,128)(2,1)} %bitcast.76, bf16[8,96,1024]{2,1,0:T(8,128)(2,1)S(1)} %bitcast.67), kind=kOutput, calls=%fused_computation.11 | convolution fusion | flops 1214251008 | bytes 15335424 | tf_op jit(solution)/shard_map/jrf,jrd->jfd/dot_general | solution.py:135
  185.2 12.0 %all-to-all-done.1 = bf16[8,96,1024]{2,1,0:T(8,128)(2,1)S(1)} async-done(((bf16[8,96,1024]{2,1,0:T(8,128)(2,1)}), bf16[8,96,1024]{2,1,0:T(8,128)(2,1)S(1)}, u32[]{:S(2)}, u32[]{:S(2)}) %all-to-all-start.1) | async-done | bytes 1572896 | tf_op jit(solution)/shard_map/all_to_all | solution.py:132
  197.2 2.7 gather_fusion
  199.9 12.8 %all-gather.5.cloned.1.call-done = bf16[768,1536]{1,0:T(8,128)(2,1)} async-done(((bf16[192,1536]{1,0:T(8,128)(2,1)}), bf16[768,1536]{1,0:T(8,128)(2,1)}) %all-gather.5.cloned.1.call-update) | async-done | bytes 2359312 | tf_op jit(solution)/shard_map/all_gather | solution.py:119
  212.7 1.8 fusion.22
  217.6 9.1 %fusion = f32[8,8,12,1024]{3,2,1,0:T(8,128)S(1)} fusion(bf16[8,8,12,768]{3,2,1,0:T(8,128)(2,1)} %reshape.133, bf16[8,1024,768]{2,1,0:T(8,128)(2,1)} %param.14), kind=kOutput, calls=%fused_computation.2 | convolution fusion | flops 1207959552 | bytes 16908288 | tf_op jit(solution)/shard_map/jscf,jdf->sjcd/dot_general | solution.py:140
  226.8 10.6 %fusion.7 = bf16[8,8,12,1024]{3,2,0,1:T(8,128)(2,1)} fusion(f32[8,8,12,1024]{3,2,1,0:T(8,128)S(1)} %fusion, bf16[8,8,12,768]{3,2,1,0:T(8,128)(2,1)} %reshape.132, bf16[8,1024,768]{2,1,0:T(8,128)(2,1)} %param.13), kind=kOutput, calls=%fused_computation.21 | convolution fusion | flops 1209532416 | bytes 18481152 | tf_op jit(solution)/shard_map/jscf,jdf->sjcd/dot_general | solution.py:139
  237.3 2.5 copy.67
  239.8 2.0 copy.68
  241.9 4.0 %all-to-all-start.3 = ((bf16[8,96,1024]{2,1,0:T(8,128)(2,1)}), bf16[8,96,1024]{2,1,0:T(8,128)(2,1)S(1)}, u32[]{:S(2)}, u32[]{:S(2)}) async-start(bf16[8,96,1024]{2,1,0:T(8,128)(2,1)} %copy.68), calls=%async_computation.4 | async-start | bytes 3145728 | tf_op jit(solution)/shard_map/all_to_all | solution.py:142
  245.8 2.4 multiply_reduce_fusion
  248.3 8.0 %convolution_convert_fusion.1 = bf16[8,1024,768]{2,1,0:T(8,128)(2,1)} fusion(bf16[8,96,1024]{2,1,0:T(8,128)(2,1)S(1)} %bitcast.62, bf16[8,96,768]{2,1,0:T(8,128)(2,1)} %bitcast.69), kind=kOutput, calls=%fused_computation.12 | convolution fusion | flops 1214251008 | bytes 15335424 | tf_op jit(solution)/shard_map/jrd,jrf->jdf/dot_general | solution.py:148
  256.3 6.6 %convolution_convert_fusion.2 = bf16[8,1024,768]{2,1,0:T(8,128)(2,1)} fusion(bf16[8,96,1024]{2,1,0:T(8,128)(2,1)S(1)} %bitcast.63, bf16[8,96,768]{2,1,0:T(8,128)(2,1)S(1)} %bitcast.68), kind=kOutput, calls=%fused_computation.13 | convolution fusion | flops 1214251008 | bytes 15335424 | tf_op jit(solution)/shard_map/jrd,jrf->jdf/dot_general | solution.py:145
  262.9 3.8 %all-to-all-done.3 = bf16[8,96,1024]{2,1,0:T(8,128)(2,1)S(1)} async-done(((bf16[8,96,1024]{2,1,0:T(8,128)(2,1)}), bf16[8,96,1024]{2,1,0:T(8,128)(2,1)S(1)}, u32[]{:S(2)}, u32[]{:S(2)}) %all-to-all-start.3) | async-done | bytes 1572896 | tf_op jit(solution)/shard_map/all_to_all | solution.py:142
  266.7 2.1 gather_fusion.1
  (75 shorter events, 19.3 us)
Async XLA Ops:
  11.3 27.3 %all-to-all-start = ((bf16[8,48,2176]{2,1,0:T(8,128)(2,1)}), bf16[8,48,2176]{2,1,0:T(8,128)(2,1)S(1)}, u32[]{:S(2)}, u32[]{:S(2)}) async-start(bf16[8,48,2176]{2,1,0:T(8,128)(2,1)} %broadcast_in_dim.60), calls=%async_computation | async-start | bytes 3342336 | tf_op jit(solution)/shard_map/all_to_all | solution.py:52
  16.5 111.7 %reduce-scatter.2.cloned.1.call-start = ((), (), s32[]{:S(2)}) async-start(), calls=%async_computation.5 | async-start | bytes 2949120 | tf_op jit(solution)/shard_map/reduce_scatter | solution.py:102
  42.2 7.4 %copy-start = (bf16[8,1024,768]{2,1,0:T(8,128)(2,1)S(1)}, bf16[8,1024,768]{2,1,0:T(8,128)(2,1)}, u32[]{:S(2)}) copy-start(bf16[8,1024,768]{2,1,0:T(8,128)(2,1)} %param.14) | copy-start | bytes 37748740
  42.3 9.4 %slice-start = ((s8[12582912]{0:T(1024)(128)(4,1)}), s8[4194304]{0:T(1024)(128)(4,1)S(1)}, s32[]{:S(2)}) async-start(s8[12582912]{0:T(1024)(128)(4,1)} %bitcast.58), calls=%async_computation.8 | async-start | bytes 8388608
  42.3 9.8 %slice-start.1 = ((s8[12582912]{0:T(1024)(128)(4,1)}), s8[4194304]{0:T(1024)(128)(4,1)S(1)}, s32[]{:S(2)}) async-start(s8[12582912]{0:T(1024)(128)(4,1)} %bitcast.58), calls=%async_computation.9 | async-start | bytes 8388608
  44.1 3.2 %copy-start.3 = (f32[768,2048]{1,0:T(8,128)}, f32[768,2048]{1,0:T(8,128)S(1)}, u32[]{:S(2)}) copy-start(f32[768,2048]{1,0:T(8,128)S(1)} %fusion.12) | copy-start | bytes 18874372
  47.6 4.1 %copy-start.1 = (bf16[768,1024]{1,0:T(8,128)(2,1)}, bf16[768,1024]{1,0:T(8,128)(2,1)S(1)}, u32[]{:S(2)}) copy-start(bf16[768,1024]{1,0:T(8,128)(2,1)S(1)} %slice.90) | copy-start | bytes 4718596
  49.6 3.8 %slice-start.2 = ((s8[12582912]{0:T(1024)(128)(4,1)}), s8[4194304]{0:T(1024)(128)(4,1)S(1)}, s32[]{:S(2)}) async-start(s8[12582912]{0:T(1024)(128)(4,1)} %bitcast.58), calls=%async_computation.10 | async-start | bytes 8388608
  57.1 103.8 %all-gather.3.cloned.1.call-start = ((), (), s32[]{:S(2)}) async-start(), calls=%async_computation.6 | async-start | bytes 1474560 | tf_op jit(solution)/shard_map/all_gather | solution.py:118
  130.5 82.1 %all-gather.5.cloned.1.call-start = ((), (), s32[]{:S(2)}) async-start(), calls=%async_computation.7 | async-start | bytes 2949120 | tf_op jit(solution)/shard_map/all_gather | solution.py:119
  172.4 3.9 %copy-start.8 = (f32[48,8]{0,1:T(8,128)S(1)}, f32[48,8]{0,1:T(8,128)}, u32[]{:S(2)}) copy-start(f32[48,8]{0,1:T(8,128)} %param.12) | copy-start | bytes 4612
  172.4 4.0 %copy-start.7 = (s32[48,8]{0,1:T(8,128)S(1)}, s32[48,8]{0,1:T(8,128)}, u32[]{:S(2)}) copy-start(s32[48,8]{0,1:T(8,128)} %param.11) | copy-start | bytes 4612
  172.4 24.8 %all-to-all-start.1 = ((bf16[8,96,1024]{2,1,0:T(8,128)(2,1)}), bf16[8,96,1024]{2,1,0:T(8,128)(2,1)S(1)}, u32[]{:S(2)}, u32[]{:S(2)}) async-start(bf16[8,96,1024]{2,1,0:T(8,128)(2,1)} %copy.63), calls=%async_computation.2 | async-start | bytes 3145728 | tf_op jit(solution)/shard_map/all_to_all | solution.py:132
  214.5 1.5 copy-start.4
  214.5 1.9 copy-start.6
  241.9 6.4 %copy-start.2 = (bf16[768,1024]{1,0:T(8,128)(2,1)S(1)}, bf16[768,1024]{1,0:T(8,128)(2,1)}, u32[]{:S(2)}) copy-start(bf16[768,1024]{1,0:T(8,128)(2,1)} %copy-done.1) | copy-start | bytes 4718596
  241.9 24.8 %all-to-all-start.3 = ((bf16[8,96,1024]{2,1,0:T(8,128)(2,1)}), bf16[8,96,1024]{2,1,0:T(8,128)(2,1)S(1)}, u32[]{:S(2)}, u32[]{:S(2)}) async-start(bf16[8,96,1024]{2,1,0:T(8,128)(2,1)} %copy.68), calls=%async_computation.4 | async-start | bytes 3145728 | tf_op jit(solution)/shard_map/all_to_all | solution.py:142
  248.3 8.0 %copy-start.5 = (bf16[768,768]{1,0:T(8,128)(2,1)S(1)}, bf16[768,768]{1,0:T(8,128)(2,1)}, u32[]{:S(2)}) copy-start(bf16[768,768]{1,0:T(8,128)(2,1)} %copy-done.4) | copy-start | bytes 3538948
Sparse Core Ops, SparseCore 0:
  57.2 66.0 reduce-scatter.1
  130.7 30.1 all-gather.2
  163.0 49.5 all-gather.4

commit v7 on v6

--- a/solution.py
+++ b/solution.py
@@ -127,8 +127,9 @@
 
     buffer_rows = experts * capacity
     expert_out = jnp.einsum(
-        "jscf,jfd->sjcd", hidden, down_weight, preferred_element_type=jnp.float32
+        "jrf,jfd->jrd", hidden.reshape(rows_shape), down_weight, preferred_element_type=jnp.float32
     ).astype(jnp.bfloat16)
+    expert_out = expert_out.reshape(local_experts, sources, capacity, width_dev).transpose(1, 0, 2, 3)
     out_back = lax.all_to_all(
         expert_out.reshape(buffer_rows, width_dev), "expert", split_axis=0, concat_axis=0, tiled=True
     )
@@ -136,9 +137,18 @@
         "jrf,jrd->jfd", hidden.reshape(rows_shape), dy_in, preferred_element_type=jnp.float32
     ).astype(jnp.bfloat16)
     expert_back = (
-        jnp.einsum("jscf,jdf->sjcd", gate_delta, gate_weight, preferred_element_type=jnp.float32)
-        + jnp.einsum("jscf,jdf->sjcd", up_delta, up_weight, preferred_element_type=jnp.float32)
+        jnp.einsum(
+            "jrf,jdf->jrd", gate_delta.reshape(rows_shape), gate_weight,
+            preferred_element_type=jnp.float32,
+        )
+        + jnp.einsum(
+            "jrf,jdf->jrd", up_delta.reshape(rows_shape), up_weight,
+            preferred_element_type=jnp.float32,
+        )
     ).astype(jnp.bfloat16)
+    expert_back = expert_back.reshape(local_experts, sources, capacity, width_dev).transpose(
+        1, 0, 2, 3
+    )
     grad_back = lax.all_to_all(
         expert_back.reshape(buffer_rows, width_dev), "expert", split_axis=0, concat_axis=0, tiled=True
     )

time: 277 us -> 273 us (0.986)
  local copies, waits for them, and re-layouts: 30.6 us -> 23 us
  matrix products: 63.4 us -> 69.5 us
    reshape x3 -> x0, local copies, waits for them, and re-layouts: 4.85 us -> none  [the longest x1 2.15 us: local(): hidden = hidden.reshape(expert_shape)]
    dot_general x1, matrix products: 1.99 us -> 6.56 us  [local(): jnp.einsum('jrd,jdf->jrf', x_in, gate_weight, preferred_element_type=jnp....]
    unnamed x26 -> x18, local copies, waits for them, and re-layouts: 7.73 us -> 4.94 us
  transfers between devices with their start and end apart: 6 -> 6, of which waited for: 5 -> 5; matrix products, arithmetic and copies ran while one was open for 19% -> 20% of each run, Pallas kernels for 0% -> 0%
where the time goes in v7:
time: 273 us; the launch traced here: 272 us
  waiting for transfers between devices  77.5 us (28%)
  matrix products  69.5 us (25%)
  blocking collectives  58.2 us (21%)
  local copies, waits for them, and re-layouts  23 us (8%)
  other arithmetic  16.6 us (6%)
  between operations  14.1 us (5%)
  starting transfers between devices  13.2 us (5%)
    all_to_all x1, blocking collectives, local(): lax.all_to_all(back_part.reshape(row_count, hidden_units), 'dp', split_ax...  58.2 us
    all_gather x1, waiting for transfers between devices, local(): hidden = lax.all_gather(hidden, 'dp', axis=0, tiled=True)  28.9 us
    all_to_all x1, waiting for transfers between devices, local(): lax.all_to_all(jnp.broadcast_to(packed[None], (sources,) + packed.shape)....  22 us
    all_gather x1, waiting for transfers between devices, local(): lax.all_gather(jnp.concatenate([gate_delta, up_delta], axis=1), 'dp', axi...  12.9 us
    dot_general x1, matrix products, local(): jnp.einsum('jrf,jrd->jfd', hidden.reshape(rows_shape), dy_in, preferred_e...  10 us
    all_to_all x1, waiting for transfers between devices, local(): lax.all_to_all(expert_out.reshape(buffer_rows, width_dev), 'expert', spli...  9.89 us
    dot_general x1, matrix products, local(): jnp.einsum('jrd,jfd->jrf', dy_in, down_weight, preferred_element_type=jnp...  9.56 us
    dot_general x1, matrix products, local(): jnp.einsum('jrf,jdf->jrd', gate_delta.reshape(rows_shape), gate_weight, p...  9.3 us
  transfers between devices with their start and end apart: 6, of which 5 were waited for; matrix products, arithmetic and copies ran while one was open for 20% of the time, Pallas kernels for 0%

profile of v7, /device:TPU:0, one launch (start us, length us, event | category | flops | bytes accessed | tf_op | source)
XLA Modules:
  0.0 272.1 jit_solution(667128261609481006)
XLA Ops:
  10.1 1.3 broadcast_in_dim.60
  11.3 5.2 %all-to-all-start = ((bf16[8,48,2176]{2,1,0:T(8,128)(2,1)}), bf16[8,48,2176]{2,1,0:T(8,128)(2,1)S(1)}, u32[]{:S(2)}, u32[]{:S(2)}) async-start(bf16[8,48,2176]{2,1,0:T(8,128)(2,1)} %broadcast_in_dim.60), calls=%async_computation | async-start | bytes 3342336 | tf_op jit(solution)/shard_map/all_to_all | solution.py:52
  16.6 22.0 %all-to-all-done = bf16[8,48,2176]{2,1,0:T(8,128)(2,1)S(1)} async-done(((bf16[8,48,2176]{2,1,0:T(8,128)(2,1)}), bf16[8,48,2176]{2,1,0:T(8,128)(2,1)S(1)}, u32[]{:S(2)}, u32[]{:S(2)}) %all-to-all-start) | async-done | bytes 1671200 | tf_op jit(solution)/shard_map/all_to_all | solution.py:52
  39.4 1.6 convert_reduce_fusion
  41.0 1.2 select_reduce_fusion.1
  42.3 1.8 fusion.1
  44.1 3.2 %copy-done.1 = f32[768,2048]{1,0:T(8,128)} copy-done((f32[768,2048]{1,0:T(8,128)}, f32[768,2048]{1,0:T(8,128)S(1)}, u32[]{:S(2)}) %copy-start.1) | copy-done | bytes 6291480
  47.5 1.6 copy-done
  49.1 2.0 convolution_convert_fusion.5
  51.1 6.6 %convolution_convert_fusion.6 = bf16[8,96,768]{2,1,0:T(8,128)(2,1)S(1)} fusion(bf16[8,96,1024]{2,1,0:T(8,128)(2,1)S(1)} %bitcast.45, bf16[8,1024,768]{2,1,0:T(8,128)(2,1)} %param.13), kind=kOutput, calls=%fused_computation.21 | convolution fusion | flops 1208549376 | bytes 15335424 | tf_op jit(solution)/shard_map/jrd,jdf->jrf/dot_general | solution.py:95
  57.7 1.6 pad_maximum_fusion
  60.9 2.1 fusion
  63.0 9.6 %convolution_convert_fusion.4 = bf16[8,96,768]{2,1,0:T(8,128)(2,1)S(1)} fusion(bf16[8,96,1024]{2,1,0:T(8,128)(2,1)S(1)} %bitcast.50, bf16[8,768,1024]{2,1,0:T(8,128)(2,1)} %param.15), kind=kOutput, calls=%fused_computation.19 | convolution fusion | flops 1208549376 | bytes 15335424 | tf_op jit(solution)/shard_map/jrd,jfd->jrf/dot_general | solution.py:103
  72.6 58.2 %all_to_all.42 = bf16[4,192,768]{2,1,0:T(8,128)(2,1)S(1)} all-to-all(bf16[4,192,768]{2,1,0:T(8,128)(2,1)S(1)} %bitcast.63), channel_id=1, replica_groups=mesh['dp'=4,'expert'=8] {'dp'}, dimensions={0} | all-to-all | bytes 2359296 | tf_op jit(solution)/shard_map/all_to_all | solution.py:107
  134.2 28.9 %all-gather.3.cloned.1.call-done = bf16[768,768]{1,0:T(8,128)(2,1)} async-done(((bf16[192,768]{1,0:T(8,128)(2,1)}), bf16[768,768]{1,0:T(8,128)(2,1)}) %all-gather.3.cloned.1.call-update) | async-done | bytes 1179664 | tf_op jit(solution)/shard_map/all_gather | solution.py:118
  163.1 7.1 %convolution_convert_fusion.3 = bf16[8,96,1024]{2,1,0:T(8,128)(2,1)S(1)} fusion(bf16[8,96,768]{2,1,0:T(8,128)(2,1)} %bitcast.64, bf16[8,768,1024]{2,1,0:T(8,128)(2,1)} %param.15), kind=kOutput, calls=%fused_computation.15 | convolution fusion | flops 1208745984 | bytes 15335424 | tf_op jit(solution)/shard_map/jrf,jfd->jrd/dot_general | solution.py:129
  171.9 2.0 copy.70
  173.9 3.9 %all-to-all-start.1 = ((bf16[8,96,1024]{2,1,0:T(8,128)(2,1)}), bf16[8,96,1024]{2,1,0:T(8,128)(2,1)S(1)}, u32[]{:S(2)}, u32[]{:S(2)}) async-start(bf16[8,96,1024]{2,1,0:T(8,128)(2,1)} %copy.70), calls=%async_computation.2 | async-start | bytes 3145728 | tf_op jit(solution)/shard_map/all_to_all | solution.py:133
  178.9 10.0 %convolution_convert_fusion = bf16[8,768,1024]{2,1,0:T(8,128)(2,1)} fusion(bf16[8,96,768]{2,1,0:T(8,128)(2,1)} %bitcast.65, bf16[8,96,1024]{2,1,0:T(8,128)(2,1)} %bitcast.51), kind=kOutput, calls=%fused_computation.5 | convolution fusion | flops 1214251008 | bytes 15335424 | tf_op jit(solution)/shard_map/jrf,jrd->jfd/dot_general | solution.py:136
  188.9 9.9 %all-to-all-done.1 = bf16[8,96,1024]{2,1,0:T(8,128)(2,1)S(1)} async-done(((bf16[8,96,1024]{2,1,0:T(8,128)(2,1)}), bf16[8,96,1024]{2,1,0:T(8,128)(2,1)S(1)}, u32[]{:S(2)}, u32[]{:S(2)}) %all-to-all-start.1) | async-done | bytes 1572896 | tf_op jit(solution)/shard_map/all_to_all | solution.py:133
  198.8 2.7 gather_fusion
  201.4 12.9 %all-gather.5.cloned.1.call-done = bf16[768,1536]{1,0:T(8,128)(2,1)} async-done(((bf16[192,1536]{1,0:T(8,128)(2,1)}), bf16[768,1536]{1,0:T(8,128)(2,1)}) %all-gather.5.cloned.1.call-update) | async-done | bytes 2359312 | tf_op jit(solution)/shard_map/all_gather | solution.py:119
  214.3 1.8 fusion.11
  216.1 9.3 %fusion.12 = f32[8,96,1024]{2,1,0:T(8,128)S(1)} fusion(bf16[8,96,768]{2,1,0:T(8,128)(2,1)S(1)} %bitcast.52, bf16[8,1024,768]{2,1,0:T(8,128)(2,1)} %param.13), kind=kOutput, calls=%fused_computation.58 | convolution fusion | flops 1207959552 | bytes 16908288 | tf_op jit(solution)/shard_map/jrf,jdf->jrd/dot_general | solution.py:140
  225.5 8.5 %add_convert_fusion = bf16[8,96,1024]{2,1,0:T(8,128)(2,1)S(1)} fusion(f32[8,96,1024]{2,1,0:T(8,128)S(1)} %fusion.12, bf16[8,96,768]{2,1,0:T(8,128)(2,1)S(1)} %bitcast.54, bf16[8,1024,768]{2,1,0:T(8,128)(2,1)} %param.14), kind=kOutput, calls=%fused_computation.12 | convolution fusion | flops 1209532416 | bytes 18481152 | tf_op jit(solution)/shard_map/jrf,jdf->jrd/dot_general | solution.py:144
  235.7 2.0 copy.76
  237.7 3.8 %all-to-all-start.3 = ((bf16[8,96,1024]{2,1,0:T(8,128)(2,1)}), bf16[8,96,1024]{2,1,0:T(8,128)(2,1)S(1)}, u32[]{:S(2)}, u32[]{:S(2)}) async-start(bf16[8,96,1024]{2,1,0:T(8,128)(2,1)} %copy.76), calls=%async_computation.4 | async-start | bytes 3145728 | tf_op jit(solution)/shard_map/all_to_all | solution.py:152
  241.6 2.4 multiply_reduce_fusion
  244.0 8.0 %convolution_convert_fusion.1 = bf16[8,1024,768]{2,1,0:T(8,128)(2,1)} fusion(bf16[8,96,1024]{2,1,0:T(8,128)(2,1)S(1)} %bitcast.46, bf16[8,96,768]{2,1,0:T(8,128)(2,1)} %bitcast.55), kind=kOutput, calls=%fused_computation.6 | convolution fusion | flops 1214251008 | bytes 15335424 | tf_op jit(solution)/shard_map/jrd,jrf->jdf/dot_general | solution.py:158
  252.0 6.6 %convolution_convert_fusion.2 = bf16[8,1024,768]{2,1,0:T(8,128)(2,1)} fusion(bf16[8,96,1024]{2,1,0:T(8,128)(2,1)S(1)} %bitcast.47, bf16[8,96,768]{2,1,0:T(8,128)(2,1)S(1)} %bitcast.53), kind=kOutput, calls=%fused_computation.7 | convolution fusion | flops 1214251008 | bytes 15335424 | tf_op jit(solution)/shard_map/jrd,jrf->jdf/dot_general | solution.py:155
  258.6 3.8 %all-to-all-done.3 = bf16[8,96,1024]{2,1,0:T(8,128)(2,1)S(1)} async-done(((bf16[8,96,1024]{2,1,0:T(8,128)(2,1)}), bf16[8,96,1024]{2,1,0:T(8,128)(2,1)S(1)}, u32[]{:S(2)}, u32[]{:S(2)}) %all-to-all-start.3) | async-done | bytes 1572896 | tf_op jit(solution)/shard_map/all_to_all | solution.py:152
  262.4 2.1 gather_fusion.1
  (65 shorter events, 14.4 us)
Async XLA Ops:
  11.3 27.3 %all-to-all-start = ((bf16[8,48,2176]{2,1,0:T(8,128)(2,1)}), bf16[8,48,2176]{2,1,0:T(8,128)(2,1)S(1)}, u32[]{:S(2)}, u32[]{:S(2)}) async-start(bf16[8,48,2176]{2,1,0:T(8,128)(2,1)} %broadcast_in_dim.60), calls=%async_computation | async-start | bytes 3342336 | tf_op jit(solution)/shard_map/all_to_all | solution.py:52
  16.5 114.5 %reduce-scatter.2.cloned.1.call-start = ((), (), s32[]{:S(2)}) async-start(), calls=%async_computation.5 | async-start | bytes 2949120 | tf_op jit(solution)/shard_map/reduce_scatter | solution.py:102
  42.2 6.9 %copy-start = (bf16[8,1024,768]{2,1,0:T(8,128)(2,1)S(1)}, bf16[8,1024,768]{2,1,0:T(8,128)(2,1)}, u32[]{:S(2)}) copy-start(bf16[8,1024,768]{2,1,0:T(8,128)(2,1)} %param.14) | copy-start | bytes 37748740
  44.1 3.2 %copy-start.1 = (f32[768,2048]{1,0:T(8,128)}, f32[768,2048]{1,0:T(8,128)S(1)}, u32[]{:S(2)}) copy-start(f32[768,2048]{1,0:T(8,128)S(1)} %fusion.1) | copy-start | bytes 18874372
  59.3 103.8 %all-gather.3.cloned.1.call-start = ((), (), s32[]{:S(2)}) async-start(), calls=%async_computation.6 | async-start | bytes 1474560 | tf_op jit(solution)/shard_map/all_gather | solution.py:118
  63.0 9.6 %copy-start.2 = (bf16[768,1024]{1,0:T(8,128)(2,1)}, bf16[768,1024]{1,0:T(8,128)(2,1)S(1)}, u32[]{:S(2)}) copy-start(bf16[768,1024]{1,0:T(8,128)(2,1)S(1)} %fusion) | copy-start | bytes 4718596
  133.3 81.0 %all-gather.5.cloned.1.call-start = ((), (), s32[]{:S(2)}) async-start(), calls=%async_computation.7 | async-start | bytes 2949120 | tf_op jit(solution)/shard_map/all_gather | solution.py:119
  173.9 3.9 %copy-start.7 = (f32[48,8]{0,1:T(8,128)S(1)}, f32[48,8]{0,1:T(8,128)}, u32[]{:S(2)}) copy-start(f32[48,8]{0,1:T(8,128)} %param.12) | copy-start | bytes 4612
  173.9 4.0 %copy-start.6 = (s32[48,8]{0,1:T(8,128)S(1)}, s32[48,8]{0,1:T(8,128)}, u32[]{:S(2)}) copy-start(s32[48,8]{0,1:T(8,128)} %param.11) | copy-start | bytes 4612
  173.9 24.8 %all-to-all-start.1 = ((bf16[8,96,1024]{2,1,0:T(8,128)(2,1)}), bf16[8,96,1024]{2,1,0:T(8,128)(2,1)S(1)}, u32[]{:S(2)}, u32[]{:S(2)}) async-start(bf16[8,96,1024]{2,1,0:T(8,128)(2,1)} %copy.70), calls=%async_computation.2 | async-start | bytes 3145728 | tf_op jit(solution)/shard_map/all_to_all | solution.py:133
  216.1 9.3 %copy-start.3 = (bf16[768,768]{1,0:T(8,128)(2,1)}, bf16[768,768]{1,0:T(8,128)(2,1)S(1)}, u32[]{:S(2)}) copy-start(bf16[768,768]{1,0:T(8,128)(2,1)S(1)} %get-tuple-element.9) | copy-start | bytes 3538948
  216.1 9.3 %copy-start.5 = (bf16[768,768]{1,0:T(8,128)(2,1)}, bf16[768,768]{1,0:T(8,128)(2,1)S(1)}, u32[]{:S(2)}) copy-start(bf16[768,768]{1,0:T(8,128)(2,1)S(1)} %get-tuple-element.8) | copy-start | bytes 3538948
  237.7 24.7 %all-to-all-start.3 = ((bf16[8,96,1024]{2,1,0:T(8,128)(2,1)}), bf16[8,96,1024]{2,1,0:T(8,128)(2,1)S(1)}, u32[]{:S(2)}, u32[]{:S(2)}) async-start(bf16[8,96,1024]{2,1,0:T(8,128)(2,1)} %copy.76), calls=%async_computation.4 | async-start | bytes 3145728 | tf_op jit(solution)/shard_map/all_to_all | solution.py:152
  244.0 8.0 %copy-start.4 = (bf16[768,768]{1,0:T(8,128)(2,1)S(1)}, bf16[768,768]{1,0:T(8,128)(2,1)}, u32[]{:S(2)}) copy-start(bf16[768,768]{1,0:T(8,128)(2,1)} %copy-done.3) | copy-start | bytes 3538948
Sparse Core Ops, SparseCore 0:
  59.4 66.0 reduce-scatter.1
  133.4 29.6 all-gather.2
  164.7 49.5 all-gather.4

commit v8 on v7

--- a/solution.py
+++ b/solution.py
@@ -165,10 +165,15 @@
     )
     slot_rank = jnp.sum(earlier_local.astype(jnp.int32), axis=1)
     slot_place = (flat_ids * capacity + slot_rank).reshape(token_count, per_token)
-    picked_out = jnp.take(out_back, slot_place, axis=0).astype(jnp.float32)
-    layer_out = jnp.sum(picked_out * route_weights[:, :, None], axis=1).astype(jnp.bfloat16)
-    picked_back = jnp.take(grad_back, slot_place, axis=0).astype(jnp.float32)
-    grad_tokens = jnp.sum(picked_back, axis=1).astype(jnp.bfloat16)
+    hit_place = slot_place[:, :, None] == jnp.arange(buffer_rows, dtype=jnp.int32)[None, None, :]
+    gather_back = jnp.sum(hit_place.astype(jnp.float32), axis=1).astype(jnp.bfloat16)
+    gather_out = jnp.sum(jnp.where(hit_place, route_weights[:, :, None], 0.0), axis=1)
+    layer_out = jnp.dot(
+        gather_out, out_back.astype(jnp.float32), precision=lax.Precision.HIGHEST
+    ).astype(jnp.bfloat16)
+    grad_tokens = jnp.dot(gather_back, grad_back, preferred_element_type=jnp.float32).astype(
+        jnp.bfloat16
+    )
     return (layer_out, grad_tokens, gate_grad, up_grad, down_grad)
 
 

time: 273 us -> 278 us (1.018)
  waiting for transfers between devices: 77.5 us -> 82.4 us
  local copies, waits for them, and re-layouts: 23 us -> 20.1 us
    all_gather x1, waiting for transfers between devices: 12.9 us -> 28.6 us  [local(): lax.all_gather(jnp.concatenate([gate_delta, up_delta], axis=1), 'dp', axi...]
    all_to_all x1, waiting for transfers between devices: 9.89 us -> 0.01 us  [local(): lax.all_to_all(expert_out.reshape(buffer_rows, width_dev), 'expert', spli...]
    dot_general x0 -> x2, matrix products: none -> 5.49 us  [the longest x1 3.05 us: local(): jnp.dot(gather_out, out_back.astype(jnp.float32), precision=lax.Precision...]
    gather x2 -> x0, local copies, waits for them, and re-layouts: 4.74 us -> none  [the longest x1 2.68 us: local(): picked_out = jnp.take(out_back, slot_place, axis=0).astype(jnp.float32)]
    unnamed x18 -> x14, local copies, waits for them, and re-layouts: 4.94 us -> 5.62 us
  transfers between devices with their start and end apart: 6 -> 6, of which waited for: 5 -> 4; matrix products, arithmetic and copies ran while one was open for 20% -> 28% of each run, Pallas kernels for 0% -> 0%
where the time goes in v8:
time: 278 us; the launch traced here: 277 us
  waiting for transfers between devices  82.4 us (30%)
  matrix products  71.6 us (26%)
  blocking collectives  58.3 us (21%)
  local copies, waits for them, and re-layouts  20.1 us (7%)
  other arithmetic  15.9 us (6%)
  starting transfers between devices  14.6 us (5%)
  between operations  14 us (5%)
    all_to_all x1, blocking collectives, local(): lax.all_to_all(back_part.reshape(row_count, hidden_units), 'dp', split_ax...  58.3 us
    all_gather x1, waiting for transfers between devices, local(): lax.all_gather(jnp.concatenate([gate_delta, up_delta], axis=1), 'dp', axi...  28.6 us
    all_gather x1, waiting for transfers between devices, local(): hidden = lax.all_gather(hidden, 'dp', axis=0, tiled=True)  27.3 us
    all_to_all x1, waiting for transfers between devices, local(): lax.all_to_all(jnp.broadcast_to(packed[None], (sources,) + packed.shape)....  22 us
    dot_general x1, matrix products, local(): jnp.einsum('jrf,jdf->jrd', up_delta.reshape(rows_shape), up_weight, prefe...  9.62 us
    dot_general x1, matrix products, local(): jnp.einsum('jrd,jfd->jrf', dy_in, down_weight, preferred_element_type=jnp...  9 us
    dot_general x1, matrix products, local(): jnp.einsum('jrf,jdf->jrd', gate_delta.reshape(rows_shape), gate_weight, p...  8.88 us
    dot_general x1, matrix products, local(): jnp.einsum('jrf,jrd->jfd', hidden.reshape(rows_shape), dy_in, preferred_e...  7.89 us
  transfers between devices with their start and end apart: 6, of which 4 were waited for; matrix products, arithmetic and copies ran while one was open for 28% of the time, Pallas kernels for 0%

profile of v8, /device:TPU:0, one launch (start us, length us, event | category | flops | bytes accessed | tf_op | source)
XLA Modules:
  0.0 276.8 jit_solution(9289735654626663154)
XLA Ops:
  11.4 1.3 broadcast_in_dim.66
  12.7 5.2 %all-to-all-start = ((bf16[8,48,2176]{2,1,0:T(8,128)(2,1)}), bf16[8,48,2176]{2,1,0:T(8,128)(2,1)S(1)}, u32[]{:S(2)}, u32[]{:S(2)}) async-start(bf16[8,48,2176]{2,1,0:T(8,128)(2,1)} %broadcast_in_dim.66), calls=%async_computation | async-start | bytes 3342336 | tf_op jit(solution)/shard_map/all_to_all | solution.py:52
  18.0 22.0 %all-to-all-done = bf16[8,48,2176]{2,1,0:T(8,128)(2,1)S(1)} async-done(((bf16[8,48,2176]{2,1,0:T(8,128)(2,1)}), bf16[8,48,2176]{2,1,0:T(8,128)(2,1)S(1)}, u32[]{:S(2)}, u32[]{:S(2)}) %all-to-all-start) | async-done | bytes 1671200 | tf_op jit(solution)/shard_map/all_to_all | solution.py:52
  40.7 1.6 convert_reduce_fusion
  43.6 1.8 fusion.1
  45.4 3.2 %copy-done.1 = f32[768,2048]{1,0:T(8,128)} copy-done((f32[768,2048]{1,0:T(8,128)}, f32[768,2048]{1,0:T(8,128)S(1)}, u32[]{:S(2)}) %copy-start.1) | copy-done | bytes 6291480
  48.9 1.6 copy-done
  50.4 2.0 convolution_convert_fusion.5
  52.5 6.6 %convolution_convert_fusion.6 = bf16[8,96,768]{2,1,0:T(8,128)(2,1)S(1)} fusion(bf16[8,96,1024]{2,1,0:T(8,128)(2,1)S(1)} %bitcast.41, bf16[8,1024,768]{2,1,0:T(8,128)(2,1)} %param.11), kind=kOutput, calls=%fused_computation.18 | convolution fusion | flops 1208549376 | bytes 15335424 | tf_op jit(solution)/shard_map/jrd,jdf->jrf/dot_general | solution.py:95
  59.0 1.6 pad_maximum_fusion
  62.2 2.1 fusion
  64.4 9.0 %convolution_convert_fusion.4 = bf16[8,96,768]{2,1,0:T(8,128)(2,1)S(1)} fusion(bf16[8,96,1024]{2,1,0:T(8,128)(2,1)S(1)} %bitcast.44, bf16[8,768,1024]{2,1,0:T(8,128)(2,1)} %param.13), kind=kOutput, calls=%fused_computation.16 | convolution fusion | flops 1208549376 | bytes 15335424 | tf_op jit(solution)/shard_map/jrd,jfd->jrf/dot_general | solution.py:103
  73.4 58.3 %all_to_all.42 = bf16[4,192,768]{2,1,0:T(8,128)(2,1)S(1)} all-to-all(bf16[4,192,768]{2,1,0:T(8,128)(2,1)S(1)} %bitcast.57), channel_id=1, replica_groups=mesh['dp'=4,'expert'=8] {'dp'}, dimensions={0} | all-to-all | bytes 2359296 | tf_op jit(solution)/shard_map/all_to_all | solution.py:107
  132.6 1.2 convert_element_type.99
  135.1 1.8 pad_maximum_fusion.1
  137.9 27.3 %all-gather.3.cloned.1.call-done = bf16[768,768]{1,0:T(8,128)(2,1)} async-done(((bf16[192,768]{1,0:T(8,128)(2,1)}), bf16[768,768]{1,0:T(8,128)(2,1)}) %all-gather.3.cloned.1.call-update) | async-done | bytes 1179664 | tf_op jit(solution)/shard_map/all_gather | solution.py:118
  165.2 7.1 %convolution_convert_fusion.3 = bf16[8,96,1024]{2,1,0:T(8,128)(2,1)S(1)} fusion(bf16[8,96,768]{2,1,0:T(8,128)(2,1)} %bitcast.58, bf16[8,768,1024]{2,1,0:T(8,128)(2,1)} %param.13), kind=kOutput, calls=%fused_computation.13 | convolution fusion | flops 1208745984 | bytes 15335424 | tf_op jit(solution)/shard_map/jrf,jfd->jrd/dot_general | solution.py:129
  174.1 2.0 copy.82
  176.1 4.5 %all-to-all-start.1 = ((bf16[8,96,1024]{2,1,0:T(8,128)(2,1)}), bf16[8,96,1024]{2,1,0:T(8,128)(2,1)}, u32[]{:S(2)}, u32[]{:S(2)}) async-start(bf16[8,96,1024]{2,1,0:T(8,128)(2,1)} %copy.82), calls=%async_computation.2 | async-start | bytes 3145728 | tf_op jit(solution)/shard_map/all_to_all | solution.py:133
  180.6 7.9 %convolution_convert_fusion = bf16[8,768,1024]{2,1,0:T(8,128)(2,1)} fusion(bf16[8,96,768]{2,1,0:T(8,128)(2,1)} %bitcast.59, bf16[8,96,1024]{2,1,0:T(8,128)(2,1)S(1)} %bitcast.45), kind=kOutput, calls=%fused_computation.3 | convolution fusion | flops 1214251008 | bytes 15335424 | tf_op jit(solution)/shard_map/jrf,jrd->jfd/dot_general | solution.py:136
  188.5 28.6 %all-gather.5.cloned.1.call-done = bf16[768,1536]{1,0:T(8,128)(2,1)} async-done(((bf16[192,1536]{1,0:T(8,128)(2,1)}), bf16[768,1536]{1,0:T(8,128)(2,1)}) %all-gather.5.cloned.1.call-update) | async-done | bytes 2359312 | tf_op jit(solution)/shard_map/all_gather | solution.py:119
  217.0 1.8 fusion.11
  218.8 8.9 %fusion.13 = f32[8,96,1024]{2,1,0:T(8,128)S(1)} fusion(bf16[8,96,768]{2,1,0:T(8,128)(2,1)S(1)} %bitcast.46, bf16[8,1024,768]{2,1,0:T(8,128)(2,1)} %param.11), kind=kOutput, calls=%fused_computation.57 | convolution fusion | flops 1207959552 | bytes 16908288 | tf_op jit(solution)/shard_map/jrf,jdf->jrd/dot_general | solution.py:140
  227.7 9.6 %add_convert_fusion = bf16[8,96,1024]{2,1,0:T(8,128)(2,1)} fusion(f32[8,96,1024]{2,1,0:T(8,128)S(1)} %fusion.13, bf16[8,96,768]{2,1,0:T(8,128)(2,1)S(1)} %bitcast.48, bf16[8,1024,768]{2,1,0:T(8,128)(2,1)} %param.12), kind=kOutput, calls=%fused_computation.10 | convolution fusion | flops 1209532416 | bytes 18481152 | tf_op jit(solution)/shard_map/jrf,jdf->jrd/dot_general | solution.py:144
  237.3 2.3 copy.83
  240.5 2.0 copy.85
  242.5 4.6 %all-to-all-start.3 = ((bf16[8,96,1024]{2,1,0:T(8,128)(2,1)}), bf16[8,96,1024]{2,1,0:T(8,128)(2,1)}, u32[]{:S(2)}, u32[]{:S(2)}) async-start(bf16[8,96,1024]{2,1,0:T(8,128)(2,1)} %copy.85), calls=%async_computation.4 | async-start | bytes 3145728 | tf_op jit(solution)/shard_map/all_to_all | solution.py:152
  247.1 3.1 %convolution_convert_fusion.8 = bf16[48,1024]{1,0:T(8,128)(2,1)} fusion(f32[48,768]{1,0:T(8,128)S(1)} %get-tuple-element.6, bf16[768,1024]{1,0:T(8,128)(2,1)} %bitcast.7), kind=kOutput, calls=%fused_computation.24 | convolution fusion | flops 453033984 | bytes 1818624 | tf_op jit(solution)/shard_map/dot_general | solution.py:171
  250.1 6.6 %convolution_convert_fusion.1 = bf16[8,1024,768]{2,1,0:T(8,128)(2,1)} fusion(bf16[8,96,1024]{2,1,0:T(8,128)(2,1)S(1)} %bitcast.42, bf16[8,96,768]{2,1,0:T(8,128)(2,1)S(1)} %bitcast.49), kind=kOutput, calls=%fused_computation.4 | convolution fusion | flops 1214251008 | bytes 15335424 | tf_op jit(solution)/shard_map/jrd,jrf->jdf/dot_general | solution.py:158
  256.8 6.6 %convolution_convert_fusion.2 = bf16[8,1024,768]{2,1,0:T(8,128)(2,1)} fusion(bf16[8,96,1024]{2,1,0:T(8,128)(2,1)S(1)} %bitcast.43, bf16[8,96,768]{2,1,0:T(8,128)(2,1)S(1)} %bitcast.47), kind=kOutput, calls=%fused_computation.5 | convolution fusion | flops 1214251008 | bytes 15335424 | tf_op jit(solution)/shard_map/jrd,jrf->jdf/dot_general | solution.py:155
  263.4 4.5 %all-to-all-done.3 = bf16[8,96,1024]{2,1,0:T(8,128)(2,1)} async-done(((bf16[8,96,1024]{2,1,0:T(8,128)(2,1)}), bf16[8,96,1024]{2,1,0:T(8,128)(2,1)}, u32[]{:S(2)}, u32[]{:S(2)}) %all-to-all-start.3) | async-done | bytes 1572896 | tf_op jit(solution)/shard_map/all_to_all | solution.py:152
  267.9 2.4 convolution_convert_fusion.7
  (56 shorter events, 13.9 us)
Async XLA Ops:
  12.7 27.3 %all-to-all-start = ((bf16[8,48,2176]{2,1,0:T(8,128)(2,1)}), bf16[8,48,2176]{2,1,0:T(8,128)(2,1)S(1)}, u32[]{:S(2)}, u32[]{:S(2)}) async-start(bf16[8,48,2176]{2,1,0:T(8,128)(2,1)} %broadcast_in_dim.66), calls=%async_computation | async-start | bytes 3342336 | tf_op jit(solution)/shard_map/all_to_all | solution.py:52
  17.9 114.8 %reduce-scatter.2.cloned.1.call-start = ((), (), s32[]{:S(2)}) async-start(), calls=%async_computation.5 | async-start | bytes 2949120 | tf_op jit(solution)/shard_map/reduce_scatter | solution.py:102
  43.6 6.9 %copy-start = (bf16[8,1024,768]{2,1,0:T(8,128)(2,1)S(1)}, bf16[8,1024,768]{2,1,0:T(8,128)(2,1)}, u32[]{:S(2)}) copy-start(bf16[8,1024,768]{2,1,0:T(8,128)(2,1)} %param.12) | copy-start | bytes 37748740
  45.4 3.2 %copy-start.1 = (f32[768,2048]{1,0:T(8,128)}, f32[768,2048]{1,0:T(8,128)S(1)}, u32[]{:S(2)}) copy-start(f32[768,2048]{1,0:T(8,128)S(1)} %fusion.1) | copy-start | bytes 18874372
  60.7 104.6 %all-gather.3.cloned.1.call-start = ((), (), s32[]{:S(2)}) async-start(), calls=%async_computation.6 | async-start | bytes 1474560 | tf_op jit(solution)/shard_map/all_gather | solution.py:118
  132.6 1.3 copy-start.4
  135.0 1.9 copy-start.5
  135.1 82.0 %all-gather.5.cloned.1.call-start = ((), (), s32[]{:S(2)}) async-start(), calls=%async_computation.7 | async-start | bytes 2949120 | tf_op jit(solution)/shard_map/all_gather | solution.py:119
  176.1 66.4 %all-to-all-start.1 = ((bf16[8,96,1024]{2,1,0:T(8,128)(2,1)}), bf16[8,96,1024]{2,1,0:T(8,128)(2,1)}, u32[]{:S(2)}, u32[]{:S(2)}) async-start(bf16[8,96,1024]{2,1,0:T(8,128)(2,1)} %copy.82), calls=%async_computation.2 | async-start | bytes 3145728 | tf_op jit(solution)/shard_map/all_to_all | solution.py:133
  218.8 8.9 %copy-start.2 = (bf16[768,768]{1,0:T(8,128)(2,1)}, bf16[768,768]{1,0:T(8,128)(2,1)S(1)}, u32[]{:S(2)}) copy-start(bf16[768,768]{1,0:T(8,128)(2,1)S(1)} %get-tuple-element.7) | copy-start | bytes 3538948
  242.5 25.4 %all-to-all-start.3 = ((bf16[8,96,1024]{2,1,0:T(8,128)(2,1)}), bf16[8,96,1024]{2,1,0:T(8,128)(2,1)}, u32[]{:S(2)}, u32[]{:S(2)}) async-start(bf16[8,96,1024]{2,1,0:T(8,128)(2,1)} %copy.85), calls=%async_computation.4 | async-start | bytes 3145728 | tf_op jit(solution)/shard_map/all_to_all | solution.py:152
  247.1 3.1 %copy-start.3 = (bf16[768,768]{1,0:T(8,128)(2,1)S(1)}, bf16[768,768]{1,0:T(8,128)(2,1)}, u32[]{:S(2)}) copy-start(bf16[768,768]{1,0:T(8,128)(2,1)} %copy-done.2) | copy-start | bytes 3538948
Sparse Core Ops, SparseCore 0:
  60.8 66.0 reduce-scatter.1
  135.2 30.0 all-gather.2
  167.4 49.5 all-gather.4

commit v9 on v7

--- a/solution.py
+++ b/solution.py
@@ -115,10 +115,19 @@
     hidden, gate_delta, up_delta = swiglu_parts(
         front_sums[:, :hidden_units], front_sums[:, hidden_units:], back_sums
     )
-    hidden = lax.all_gather(hidden, "dp", axis=0, tiled=True)
-    deltas = lax.all_gather(
-        jnp.concatenate([gate_delta, up_delta], axis=1), "dp", axis=0, tiled=True
-    )
+    def dp_gather(block):
+        return lax.all_to_all(
+            jnp.broadcast_to(block[None], (dp_count,) + block.shape).reshape(
+                dp_count * block.shape[0], block.shape[1]
+            ),
+            "dp",
+            split_axis=0,
+            concat_axis=0,
+            tiled=True,
+        )
+
+    hidden = dp_gather(hidden)
+    deltas = dp_gather(jnp.concatenate([gate_delta, up_delta], axis=1))
     expert_shape = (local_experts, sources, capacity, hidden_units)
     hidden = hidden.reshape(expert_shape)
     gate_delta = deltas[:, :hidden_units].reshape(expert_shape)

time: 273 us -> 319 us (1.17)
  blocking collectives: 58.2 us -> 89.7 us
  waiting for transfers between devices: 77.5 us -> 82.9 us
  starting transfers between devices: 13.2 us -> 18.3 us
    all_gather x2 -> x0, waiting for transfers between devices: 41.8 us -> none  [the longest x1 28.9 us: local(): hidden = lax.all_gather(hidden, 'dp', axis=0, tiled=True)]
    all_to_all x0 -> x1, waiting for transfers between devices: none -> 37.7 us  [dp_gather(): lax.all_to_all(jnp.broadcast_to(block[None], (dp_count,) + block.shape).r...]
    all_to_all x0 -> x1, blocking collectives: none -> 31.5 us  [dp_gather(): lax.all_to_all(jnp.broadcast_to(block[None], (dp_count,) + block.shape).r...]
    all_to_all x1, waiting for transfers between devices: 9.89 us -> 19.2 us  [local(): lax.all_to_all(expert_out.reshape(buffer_rows, width_dev), 'expert', spli...]
    all_to_all x0 -> x1, starting transfers between devices: none -> 4.62 us  [dp_gather(): lax.all_to_all(jnp.broadcast_to(block[None], (dp_count,) + block.shape).r...]
  transfers between devices with their start and end apart: 6 -> 5, of which waited for: 5 -> 4; matrix products, arithmetic and copies ran while one was open for 20% -> 14% of each run, Pallas kernels for 0% -> 0%
where the time goes in v9:
time: 319 us; the launch traced here: 318 us
  blocking collectives  89.7 us (28%)
  waiting for transfers between devices  82.9 us (26%)
  matrix products  69.6 us (22%)
  local copies, waits for them, and re-layouts  25.7 us (8%)
  starting transfers between devices  18.3 us (6%)
  other arithmetic  17.6 us (6%)
  between operations  14.4 us (5%)
    all_to_all x1, blocking collectives, local(): lax.all_to_all(back_part.reshape(row_count, hidden_units), 'dp', split_ax...  58.2 us
    all_to_all x1, waiting for transfers between devices, dp_gather(): lax.all_to_all(jnp.broadcast_to(block[None], (dp_count,) + block.shape).r...  37.7 us
    all_to_all x1, blocking collectives, dp_gather(): lax.all_to_all(jnp.broadcast_to(block[None], (dp_count,) + block.shape).r...  31.5 us
    all_to_all x1, waiting for transfers between devices, local(): lax.all_to_all(jnp.broadcast_to(packed[None], (sources,) + packed.shape)....  22 us
    all_to_all x1, waiting for transfers between devices, local(): lax.all_to_all(expert_out.reshape(buffer_rows, width_dev), 'expert', spli...  19.2 us
    dot_general x1, matrix products, local(): jnp.einsum('jrf,jrd->jfd', hidden.reshape(rows_shape), dy_in, preferred_e...  10 us
    dot_general x1, matrix products, local(): jnp.einsum('jrd,jfd->jrf', dy_in, down_weight, preferred_element_type=jnp...  9.58 us
    dot_general x1, matrix products, local(): jnp.einsum('jrf,jdf->jrd', gate_delta.reshape(rows_shape), gate_weight, p...  9.31 us
  transfers between devices with their start and end apart: 5, of which 4 were waited for; matrix products, arithmetic and copies ran while one was open for 14% of the time, Pallas kernels for 0%

profile of v9, /device:TPU:0, one launch (start us, length us, event | category | flops | bytes accessed | tf_op | source)
XLA Modules:
  0.0 318.2 jit_solution(10906606119983655917)
XLA Ops:
  11.3 5.2 %all-to-all-start = ((bf16[8,48,2176]{2,1,0:T(8,128)(2,1)}), bf16[8,48,2176]{2,1,0:T(8,128)(2,1)S(1)}, u32[]{:S(2)}, u32[]{:S(2)}) async-start(bf16[8,48,2176]{2,1,0:T(8,128)(2,1)} %broadcast_in_dim.72), calls=%async_computation | async-start | bytes 3342336 | tf_op jit(solution)/shard_map/all_to_all | solution.py:52
  16.6 22.0 %all-to-all-done = bf16[8,48,2176]{2,1,0:T(8,128)(2,1)S(1)} async-done(((bf16[8,48,2176]{2,1,0:T(8,128)(2,1)}), bf16[8,48,2176]{2,1,0:T(8,128)(2,1)S(1)}, u32[]{:S(2)}, u32[]{:S(2)}) %all-to-all-start) | async-done | bytes 1671200 | tf_op jit(solution)/shard_map/all_to_all | solution.py:52
  39.4 1.6 convert_reduce_fusion
  42.3 1.8 fusion.1
  44.1 3.2 %copy-done.1 = f32[768,2048]{1,0:T(8,128)} copy-done((f32[768,2048]{1,0:T(8,128)}, f32[768,2048]{1,0:T(8,128)S(1)}, u32[]{:S(2)}) %copy-start.1) | copy-done | bytes 6291480
  49.1 2.0 convolution_convert_fusion.5
  51.1 6.6 %convolution_convert_fusion.6 = bf16[8,96,768]{2,1,0:T(8,128)(2,1)S(1)} fusion(bf16[8,96,1024]{2,1,0:T(8,128)(2,1)S(1)} %bitcast.46, bf16[8,1024,768]{2,1,0:T(8,128)(2,1)} %param.13), kind=kOutput, calls=%fused_computation.21 | convolution fusion | flops 1208549376 | bytes 15335424 | tf_op jit(solution)/shard_map/jrd,jdf->jrf/dot_general | solution.py:95
  57.7 1.6 pad_maximum_fusion
  60.7 2.1 fusion
  62.8 9.6 %convolution_convert_fusion.4 = bf16[8,96,768]{2,1,0:T(8,128)(2,1)S(1)} fusion(bf16[8,96,1024]{2,1,0:T(8,128)(2,1)S(1)} %bitcast.51, bf16[8,768,1024]{2,1,0:T(8,128)(2,1)} %param.15), kind=kOutput, calls=%fused_computation.19 | convolution fusion | flops 1208549376 | bytes 15335424 | tf_op jit(solution)/shard_map/jrd,jfd->jrf/dot_general | solution.py:103
  72.4 58.2 %all_to_all.57 = bf16[4,192,768]{2,1,0:T(8,128)(2,1)S(1)} all-to-all(bf16[4,192,768]{2,1,0:T(8,128)(2,1)S(1)} %bitcast.66), channel_id=1, replica_groups=mesh['dp'=4,'expert'=8] {'dp'}, dimensions={0} | all-to-all | bytes 2359296 | tf_op jit(solution)/shard_map/all_to_all | solution.py:107
  133.2 31.5 %all_to_all.58 = bf16[4,192,768]{2,1,0:T(8,128)(2,1)S(1)} all-to-all(bf16[4,192,768]{2,1,0:T(8,128)(2,1)S(1)} %broadcast_in_dim.76), channel_id=1, replica_groups=mesh['dp'=4,'expert'=8] {'dp'}, dimensions={0} | all-to-all | bytes 2359296 | tf_op jit(solution)/shard_map/all_to_all | solution.py:119
  164.7 7.2 %convolution_convert_fusion.3 = bf16[8,96,1024]{2,1,0:T(8,128)(2,1)S(1)} fusion(bf16[8,96,768]{2,1,0:T(8,128)(2,1)S(1)} %bitcast.57, bf16[8,768,1024]{2,1,0:T(8,128)(2,1)} %param.15), kind=kOutput, calls=%fused_computation.15 | convolution fusion | flops 1208745984 | bytes 15335424 | tf_op jit(solution)/shard_map/jrf,jfd->jrd/dot_general | solution.py:138
  173.6 2.0 copy.70
  175.7 3.7 %all-to-all-start.2 = ((bf16[8,96,1024]{2,1,0:T(8,128)(2,1)}), bf16[8,96,1024]{2,1,0:T(8,128)(2,1)S(1)}, u32[]{:S(2)}, u32[]{:S(2)}) async-start(bf16[8,96,1024]{2,1,0:T(8,128)(2,1)} %copy.70), calls=%async_computation.3 | async-start | bytes 3145728 | tf_op jit(solution)/shard_map/all_to_all | solution.py:142
  179.3 1.8 pad_maximum_fusion.1
  181.1 19.2 %all-to-all-done.2 = bf16[8,96,1024]{2,1,0:T(8,128)(2,1)S(1)} async-done(((bf16[8,96,1024]{2,1,0:T(8,128)(2,1)}), bf16[8,96,1024]{2,1,0:T(8,128)(2,1)S(1)}, u32[]{:S(2)}, u32[]{:S(2)}) %all-to-all-start.2) | async-done | bytes 1572896 | tf_op jit(solution)/shard_map/all_to_all | solution.py:142
  200.3 2.6 broadcast_in_dim.80
  203.0 4.6 %all-to-all-start.4 = ((bf16[4,192,1536]{2,1,0:T(8,128)(2,1)}), bf16[4,192,1536]{2,1,0:T(8,128)(2,1)}, u32[]{:S(2)}, u32[]{:S(2)}) async-start(bf16[4,192,1536]{2,1,0:T(8,128)(2,1)} %broadcast_in_dim.80), calls=%async_computation.5 | async-start | bytes 4718592 | tf_op jit(solution)/shard_map/all_to_all | solution.py:119
  208.6 10.0 %convolution_convert_fusion = bf16[8,768,1024]{2,1,0:T(8,128)(2,1)} fusion(bf16[8,96,768]{2,1,0:T(8,128)(2,1)} %bitcast.58, bf16[8,96,1024]{2,1,0:T(8,128)(2,1)} %bitcast.52), kind=kOutput, calls=%fused_computation.5 | convolution fusion | flops 1214251008 | bytes 15335424 | tf_op jit(solution)/shard_map/jrf,jrd->jfd/dot_general | solution.py:145
  218.6 2.7 gather_fusion
  221.3 37.7 %all-to-all-done.4 = bf16[4,192,1536]{2,1,0:T(8,128)(2,1)} async-done(((bf16[4,192,1536]{2,1,0:T(8,128)(2,1)}), bf16[4,192,1536]{2,1,0:T(8,128)(2,1)}, u32[]{:S(2)}, u32[]{:S(2)}) %all-to-all-start.4) | async-done | bytes 2359328 | tf_op jit(solution)/shard_map/all_to_all | solution.py:119
  259.0 1.8 fusion.11
  260.8 9.3 %fusion.12 = f32[8,96,1024]{2,1,0:T(8,128)S(1)} fusion(bf16[8,96,768]{2,1,0:T(8,128)(2,1)S(1)} %bitcast.53, bf16[8,1024,768]{2,1,0:T(8,128)(2,1)} %param.13), kind=kOutput, calls=%fused_computation.58 | convolution fusion | flops 1207959552 | bytes 16908288 | tf_op jit(solution)/shard_map/jrf,jdf->jrd/dot_general | solution.py:149
  270.1 8.5 %add_convert_fusion = bf16[8,96,1024]{2,1,0:T(8,128)(2,1)S(1)} fusion(f32[8,96,1024]{2,1,0:T(8,128)S(1)} %fusion.12, bf16[8,96,768]{2,1,0:T(8,128)(2,1)S(1)} %bitcast.55, bf16[8,1024,768]{2,1,0:T(8,128)(2,1)} %param.14), kind=kOutput, calls=%fused_computation.12 | convolution fusion | flops 1209532416 | bytes 18481152 | tf_op jit(solution)/shard_map/jrf,jdf->jrd/dot_general | solution.py:153
  280.4 2.0 copy.76
  282.4 4.8 %all-to-all-start.5 = ((bf16[8,96,1024]{2,1,0:T(8,128)(2,1)}), bf16[8,96,1024]{2,1,0:T(8,128)(2,1)S(1)}, u32[]{:S(2)}, u32[]{:S(2)}) async-start(bf16[8,96,1024]{2,1,0:T(8,128)(2,1)} %copy.76), calls=%async_computation.6 | async-start | bytes 3145728 | tf_op jit(solution)/shard_map/all_to_all | solution.py:161
  287.2 2.4 multiply_reduce_fusion
  289.6 8.0 %convolution_convert_fusion.1 = bf16[8,1024,768]{2,1,0:T(8,128)(2,1)} fusion(bf16[8,96,1024]{2,1,0:T(8,128)(2,1)S(1)} %bitcast.47, bf16[8,96,768]{2,1,0:T(8,128)(2,1)} %bitcast.56), kind=kOutput, calls=%fused_computation.6 | convolution fusion | flops 1214251008 | bytes 15335424 | tf_op jit(solution)/shard_map/jrd,jrf->jdf/dot_general | solution.py:167
  297.6 6.6 %convolution_convert_fusion.2 = bf16[8,1024,768]{2,1,0:T(8,128)(2,1)} fusion(bf16[8,96,1024]{2,1,0:T(8,128)(2,1)S(1)} %bitcast.48, bf16[8,96,768]{2,1,0:T(8,128)(2,1)S(1)} %bitcast.54), kind=kOutput, calls=%fused_computation.7 | convolution fusion | flops 1214251008 | bytes 15335424 | tf_op jit(solution)/shard_map/jrd,jrf->jdf/dot_general | solution.py:164
  304.2 4.0 %all-to-all-done.5 = bf16[8,96,1024]{2,1,0:T(8,128)(2,1)S(1)} async-done(((bf16[8,96,1024]{2,1,0:T(8,128)(2,1)}), bf16[8,96,1024]{2,1,0:T(8,128)(2,1)S(1)}, u32[]{:S(2)}, u32[]{:S(2)}) %all-to-all-start.5) | async-done | bytes 1572896 | tf_op jit(solution)/shard_map/all_to_all | solution.py:161
  308.2 2.1 gather_fusion.1
  (66 shorter events, 17.4 us)
Async XLA Ops:
  11.3 27.3 %all-to-all-start = ((bf16[8,48,2176]{2,1,0:T(8,128)(2,1)}), bf16[8,48,2176]{2,1,0:T(8,128)(2,1)S(1)}, u32[]{:S(2)}, u32[]{:S(2)}) async-start(bf16[8,48,2176]{2,1,0:T(8,128)(2,1)} %broadcast_in_dim.72), calls=%async_computation | async-start | bytes 3342336 | tf_op jit(solution)/shard_map/all_to_all | solution.py:52
  16.5 114.3 %reduce-scatter.2.cloned.1.call-start = ((), (), s32[]{:S(2)}) async-start(), calls=%async_computation.7 | async-start | bytes 2949120 | tf_op jit(solution)/shard_map/reduce_scatter | solution.py:102
  42.2 6.9 %copy-start = (bf16[8,1024,768]{2,1,0:T(8,128)(2,1)S(1)}, bf16[8,1024,768]{2,1,0:T(8,128)(2,1)}, u32[]{:S(2)}) copy-start(bf16[8,1024,768]{2,1,0:T(8,128)(2,1)} %param.14) | copy-start | bytes 37748740
  44.1 3.2 %copy-start.1 = (f32[768,2048]{1,0:T(8,128)}, f32[768,2048]{1,0:T(8,128)S(1)}, u32[]{:S(2)}) copy-start(f32[768,2048]{1,0:T(8,128)S(1)} %fusion.1) | copy-start | bytes 18874372
  62.8 9.6 %copy-start.2 = (bf16[768,1024]{1,0:T(8,128)(2,1)}, bf16[768,1024]{1,0:T(8,128)(2,1)S(1)}, u32[]{:S(2)}) copy-start(bf16[768,1024]{1,0:T(8,128)(2,1)S(1)} %fusion) | copy-start | bytes 4718596
  164.7 7.2 %copy-start.6 = (bf16[4,192,768]{2,1,0:T(8,128)(2,1)}, bf16[4,192,768]{2,1,0:T(8,128)(2,1)S(1)}, u32[]{:S(2)}) copy-start(bf16[4,192,768]{2,1,0:T(8,128)(2,1)S(1)} %all_to_all.58) | copy-start | bytes 3538948
  175.7 24.7 %all-to-all-start.2 = ((bf16[8,96,1024]{2,1,0:T(8,128)(2,1)}), bf16[8,96,1024]{2,1,0:T(8,128)(2,1)S(1)}, u32[]{:S(2)}, u32[]{:S(2)}) async-start(bf16[8,96,1024]{2,1,0:T(8,128)(2,1)} %copy.70), calls=%async_computation.3 | async-start | bytes 3145728 | tf_op jit(solution)/shard_map/all_to_all | solution.py:142
  203.0 4.6 %copy-start.8 = (f32[48,8]{0,1:T(8,128)S(1)}, f32[48,8]{0,1:T(8,128)}, u32[]{:S(2)}) copy-start(f32[48,8]{0,1:T(8,128)} %param.12) | copy-start | bytes 4612
  203.0 4.7 %copy-start.7 = (s32[48,8]{0,1:T(8,128)S(1)}, s32[48,8]{0,1:T(8,128)}, u32[]{:S(2)}) copy-start(s32[48,8]{0,1:T(8,128)} %param.11) | copy-start | bytes 4612
  203.0 56.0 %all-to-all-start.4 = ((bf16[4,192,1536]{2,1,0:T(8,128)(2,1)}), bf16[4,192,1536]{2,1,0:T(8,128)(2,1)}, u32[]{:S(2)}, u32[]{:S(2)}) async-start(bf16[4,192,1536]{2,1,0:T(8,128)(2,1)} %broadcast_in_dim.80), calls=%async_computation.5 | async-start | bytes 4718592 | tf_op jit(solution)/shard_map/all_to_all | solution.py:119
  260.8 9.3 %copy-start.3 = (bf16[768,768]{1,0:T(8,128)(2,1)}, bf16[768,768]{1,0:T(8,128)(2,1)S(1)}, u32[]{:S(2)}) copy-start(bf16[768,768]{1,0:T(8,128)(2,1)S(1)} %get-tuple-element.9) | copy-start | bytes 3538948
  260.8 9.3 %copy-start.5 = (bf16[768,768]{1,0:T(8,128)(2,1)}, bf16[768,768]{1,0:T(8,128)(2,1)S(1)}, u32[]{:S(2)}) copy-start(bf16[768,768]{1,0:T(8,128)(2,1)S(1)} %get-tuple-element.8) | copy-start | bytes 3538948
  282.4 25.8 %all-to-all-start.5 = ((bf16[8,96,1024]{2,1,0:T(8,128)(2,1)}), bf16[8,96,1024]{2,1,0:T(8,128)(2,1)S(1)}, u32[]{:S(2)}, u32[]{:S(2)}) async-start(bf16[8,96,1024]{2,1,0:T(8,128)(2,1)} %copy.76), calls=%async_computation.6 | async-start | bytes 3145728 | tf_op jit(solution)/shard_map/all_to_all | solution.py:161
  289.6 8.0 %copy-start.4 = (bf16[768,768]{1,0:T(8,128)(2,1)S(1)}, bf16[768,768]{1,0:T(8,128)(2,1)}, u32[]{:S(2)}) copy-start(bf16[768,768]{1,0:T(8,128)(2,1)} %copy-done.3) | copy-start | bytes 3538948
Sparse Core Ops, SparseCore 0:
  59.4 66.0 reduce-scatter.1
